TPU v7x, 1024 devices: a whole 4x8x16 slice. The times are simulated.
1024 devices in a mesh: tile: 64 (over x, y, core), chan: 16 (over z).
Axes of the slice: x: 4, y: 8, z: 16, core: 2. Of those that a mesh axis runs over, the one named last changes fastest.
Arguments:
- points: bfloat16 [128, 65536], P('chan', 'tile'), may hold values from -6 to 6
- dest: int32 [65536, 1], P('tile'), may hold values from 0 to 63; in each aligned block of 1024 rows (0 to 1023, 1024 to 2047, ...) at most 48 rows name the same one
- voxel: int32 [65536, 1], P('tile'), may hold values from 0 to 2047
- weight: bfloat16 [256, 27, 128], P('chan'), may hold values from -0.109375 to 0.109375
- grad_out: bfloat16 [256, 131072], P('chan', 'tile'), may hold values from -6 to 6
Outputs:
- features_out: bfloat16 [256, 131072], P('chan', 'tile')
- weight_grad: float32 [256, 3456], P('chan', 'tile')
Inputs may be any that keep to these rules, and one draw needn't show every extreme that they name: `dest`: among the 1024 points of one scene owner (aligned blocks of rows), at most 48 go to any one tile, and some tile receives exactly 48 of them.
All inputs are finite; a program needn't handle non-finite values.
Results may differ from a plain program's by a relative error of at most 0.0029.
Values may be sent and summed in bfloat16 or wider, within the bound.
No kernel may reach another device: no remote copies, remote signals or barrier semaphores. Data moves between devices by JAX's collectives and lax.ppermute only.
A program may use at most 64 MiB of HBM per device.

v0:
```python
import jax
import jax.numpy as jnp
import numpy as np
from jax import lax
from jax.sharding import Mesh
from jax.sharding import PartitionSpec as P

C_IN = 128
EDGE = 16
DEPTH = 8
VOX = 2048
OFFSETS = [(k // 9 - 1, k // 3 % 3 - 1, k % 3 - 1) for k in range(27)]
TILE_AXES = ("tx", "ty", "tc")


REACH = 256 + 16 + 1


def valid(a, b, e):
    v = lax.broadcasted_iota(jnp.int32, (1, VOX), 1)
    i, j, l = v // (EDGE * EDGE), v // EDGE % EDGE, v % EDGE
    return (
        (i + a >= 0) & (i + a < DEPTH) & (j + b >= 0) & (j + b < EDGE) & (l + e >= 0) & (l + e < EDGE)
    )


def shifted(padded, k, signs):
    a, b, e = (signs * x for x in OFFSETS[k])
    d = (a * EDGE + b) * EDGE + e
    part = padded[:, REACH + d : REACH + d + VOX]
    return jnp.where(valid(a, b, e), part, jnp.zeros_like(part))


def on_device(tiles, points, dest, voxel, weight, grad_out):
    count = dest.shape[0]
    capacity = min(count, 3 * count // tiles)
    slots = tiles * capacity
    out_rows = weight.shape[0]
    channels = points.shape[0]

    onehot = (dest == jnp.arange(tiles, dtype=jnp.int32)[None, :]).astype(jnp.bfloat16)
    rows = jnp.arange(count, dtype=jnp.int32)
    earlier = (rows[:, None] > rows[None, :]).astype(jnp.bfloat16)
    before = jnp.dot(earlier, onehot, preferred_element_type=jnp.float32)
    rank = jnp.sum(before * onehot.astype(jnp.float32), axis=1).astype(jnp.int32)
    place = dest[:, 0] * capacity + rank

    vox = voxel[:, 0]
    codes = jnp.stack([vox // 64 + 1, vox % 64]).astype(jnp.bfloat16)
    payload = jnp.concatenate([points, codes], axis=0)
    select = (place[:, None] == jnp.arange(slots, dtype=jnp.int32)[None, :]).astype(jnp.bfloat16)
    send = jnp.dot(payload, select, preferred_element_type=jnp.float32).astype(jnp.bfloat16)
    received = lax.all_to_all(send, TILE_AXES, split_axis=1, concat_axis=1, tiled=True)

    high = received[channels].astype(jnp.int32)
    low = received[channels + 1].astype(jnp.int32)
    cell = jnp.where(high > 0, (high - 1) * 64 + low, VOX)
    member = (cell[:, None] == jnp.arange(VOX, dtype=jnp.int32)[None, :]).astype(jnp.bfloat16)
    summed = jnp.concatenate(
        [received[:channels], jnp.ones((1, slots), jnp.bfloat16)], axis=0
    )
    sums = jnp.dot(summed, member, preferred_element_type=jnp.float32)
    counts = sums[channels]
    grid = (sums[:channels] / jnp.maximum(counts, 1.0)[None, :]).astype(jnp.bfloat16)
    occupied = (counts > 0).astype(jnp.float32)

    full = lax.all_gather(grid, "chan", axis=0, tiled=True)
    masked = (grad_out.astype(jnp.float32) * occupied[None, :]).astype(jnp.bfloat16)

    stacked_w = weight.transpose(1, 0, 2).reshape(27 * out_rows, C_IN)
    wide = jnp.pad(full, ((0, 0), (REACH, REACH)))
    partial = jnp.dot(stacked_w, wide, preferred_element_type=jnp.float32)
    output = None
    for k in range(27):
        part = shifted(partial[k * out_rows : (k + 1) * out_rows], k, 1)
        output = part if output is None else output + part
    features_out = (output * occupied[None, :]).astype(jnp.bfloat16)

    wide_masked = jnp.pad(masked, ((0, 0), (REACH, REACH)))
    moved = jnp.stack([shifted(wide_masked, k, -1) for k in range(27)]).reshape(27 * out_rows, VOX)
    grads = lax.dot_general(
        moved, full, (((1,), (1,)), ((), ())), preferred_element_type=jnp.float32
    )
    grads = grads.reshape(27, out_rows, C_IN).transpose(1, 0, 2).reshape(out_rows, 27 * C_IN)
    width = grads.shape[1] // tiles
    chunks = grads.reshape(out_rows, tiles, width).transpose(1, 0, 2)
    arrived = lax.all_to_all(chunks, TILE_AXES, split_axis=0, concat_axis=0, tiled=True)
    weight_grad = jnp.sum(arrived, axis=0)
    return (features_out, weight_grad)


def solution(mesh):
    tiles, chans = mesh.devices.shape
    split = Mesh(mesh.devices.reshape(4, tiles // 8, 2, chans), (*TILE_AXES, "chan"))
    tile = TILE_AXES
    placed = (
        P("chan", tile),
        P(tile, None),
        P(tile, None),
        P("chan", None, None),
        P("chan", tile),
    )

    def step(*args):
        return on_device(tiles, *args)

    return jax.shard_map(
        step,
        mesh=split,
        in_specs=placed,
        out_specs=(P("chan", tile), P("chan", tile)),
        check_vma=False,
    )
```

profile of v0, /device:TPU:1, one launch (start us, length us, event | category | flops | bytes accessed | tf_op | source)
XLA Modules:
  0.0 103.9 jit_solution(13168499985956033826)
XLA Ops:
  0.6 1.4 %fusion.7 = f32[1024]{0:T(1024)S(1)} fusion(s32[1024]{0:T(1024)} %bitcast.152), kind=kOutput, calls=%fused_computation.12 | convolution fusion | flops 135658496 | bytes 8192 | tf_op jit(solution)/shard_map/dot_general | solution.py:44
  2.0 0.7 multiply_add_fusion
  2.7 0.7 add_convert_fusion
  3.5 3.1 %fusion.5 = bf16[10,3072]{1,0:T(8,128)(2,1)S(1)} fusion(s32[1024]{0:T(1024)S(1)} %bitcast.153, bf16[1,1024]{1,0:T(2,128)(2,1)S(1)} %fusion.156, bf16[1,1024]{1,0:T(2,128)(2,1)S(1)} %get-tuple-element.2, bf16[8,1024]{1,0:T(8,128)(2,1)} %param.5), kind=kOutput, calls=%fused_computation.9 | convolution fusion | flops 66152448 | bytes 86016 | tf_op jit(solution)/shard_map/dot_general | solution.py:52
  6.5 0.2 all_to_all.9
  6.7 0.1 copy.13
  6.8 0.8 reshape.490
  7.7 18.2 %all-to-all-start = ((bf16[64,2,240]{2,1,0:T(2,128)(2,1)}), bf16[64,2,240]{2,1,0:T(2,128)(2,1)S(1)}, u32[]{:S(2)}, u32[]{:S(2)}) async-start(bf16[64,2,240]{2,1,0:T(2,128)(2,1)} %reshape.490), calls=%async_computation | async-start | bytes 131072 | tf_op jit(solution)/shard_map/all_to_all | solution.py:53
  26.1 9.6 %all-to-all-done = bf16[64,2,240]{2,1,0:T(2,128)(2,1)S(1)} async-done(((bf16[64,2,240]{2,1,0:T(2,128)(2,1)}), bf16[64,2,240]{2,1,0:T(2,128)(2,1)S(1)}, u32[]{:S(2)}, u32[]{:S(2)}) %all-to-all-start) | async-done | bytes 61472 | tf_op jit(solution)/shard_map/all_to_all | solution.py:53
  35.8 0.2 reshape.491
  36.0 0.2 fusion.120
  36.3 0.2 slice.235
  36.5 4.4 %fusion = f32[9,2048]{1,0:T(8,128)S(1)} fusion(s32[3072]{0:T(1024)S(1)} %reshape.480, bf16[8,3072]{1,0:T(8,128)(2,1)S(1)} %slice.235), kind=kOutput, calls=%fused_computation.1 | convolution fusion | flops 119537664 | bytes 135168 | tf_op jit(solution)/shard_map/dot_general | solution.py:62
  41.0 32.0 %all_gather.3 = bf16[128,2048]{1,0:T(8,128)(2,1)S(1)} all-gather(bf16[8,2048]{1,0:T(8,128)(2,1)S(1)} %fusion.119), channel_id=1, replica_groups=mesh['tx'=4,'ty'=8,'tc'=2,'chan'=16] {'chan'}, dimensions={0}, use_global_device_ids=true | all-gather | bytes 557056 | tf_op jit(solution)/shard_map/all_gather | solution.py:67
  73.8 0.1 fusion.70
  73.9 0.1 fusion.73
  74.0 0.1 fusion.76
  74.1 0.1 fusion.79
  74.2 0.1 fusion.82
  74.5 0.1 fusion.91
  75.3 0.7 convolution_bitcast_fusion.1
  76.1 0.7 reshape_reshape.3
  76.8 0.3 copy.11
  77.2 1.2 %reshape.492 = f32[64,1,864]{2,1,0:T(1,128)} reshape(f32[64,16,54]{2,1,0:T(8,128)S(1)} %copy.11) | data formatting | bytes 442368
  78.4 11.5 %all-to-all-start.1 = ((f32[64,1,864]{2,1,0:T(1,128)}), f32[64,1,864]{2,1,0:T(1,128)S(1)}, u32[]{:S(2)}, u32[]{:S(2)}) async-start(f32[64,1,864]{2,1,0:T(1,128)} %reshape.492), calls=%async_computation.1 | async-start | bytes 458752 | tf_op jit(solution)/shard_map/all_to_all | solution.py:87
  89.9 0.8 convolution_bitcast_fusion
  90.6 1.6 %fusion.13 = bf16[16,2048]{1,0:T(8,128)(2,1)} fusion(f32[432,2594]{1,0:T(8,128)S(1)} %convolution_bitcast_fusion, f32[2048]{0:T(1024)S(1)} %bitcast.149, pred[2048]{0:T(1024)(128)(4,1)S(1)} %get-tuple-element.4, pred[2048]{0:T(1024)(128)(4,1)S(1)} %get-tuple-element.5, pred[2048]{0:T(1024)(128)(4,1)S(1)} %get-tuple-element.6, ...), kind=kLoop, calls=%fused_computation.20 | loop fusion | flops 1802240 | bytes 3667968 | tf_op jit(solution)/shard_map/convert_element_type | solution.py:77
  92.3 8.9 %all-to-all-done.1 = f32[64,1,864]{2,1,0:T(1,128)S(1)} async-done(((f32[64,1,864]{2,1,0:T(1,128)}), f32[64,1,864]{2,1,0:T(1,128)S(1)}, u32[]{:S(2)}, u32[]{:S(2)}) %all-to-all-start.1) | async-done | bytes 221216 | tf_op jit(solution)/shard_map/all_to_all | solution.py:87
  101.1 0.5 broadcast.2887
  101.6 1.2 %reduce.4 = f32[64,864]{1,0:T(8,128)S(1)} reduce(f32[64,1,864]{2,1,0:T(1,128)S(1)} %all-to-all-done.1, f32[]{:T(128)} %broadcast.2887), dimensions={1}, to_apply=%all_to_all.11.reduce_sub_computation | reduce | bytes 442372 | tf_op jit(solution)/shard_map/all_to_all | solution.py:87
  102.8 0.4 reshape.493
  103.2 0.7 reduce_sum.19
  (49 shorter events, 2.1 us)
Async XLA Ops:
  0.6 89.2 %copy-start = (bf16[16,27,128]{2,0,1:T(8,128)(2,1)S(1)}, bf16[16,27,128]{2,0,1:T(8,128)(2,1)}, u32[]{:S(2)}) copy-start(bf16[16,27,128]{2,0,1:T(8,128)(2,1)} %param.8) | copy-start | bytes 331780
  7.7 28.1 %all-to-all-start = ((bf16[64,2,240]{2,1,0:T(2,128)(2,1)}), bf16[64,2,240]{2,1,0:T(2,128)(2,1)S(1)}, u32[]{:S(2)}, u32[]{:S(2)}) async-start(bf16[64,2,240]{2,1,0:T(2,128)(2,1)} %reshape.490), calls=%async_computation | async-start | bytes 131072 | tf_op jit(solution)/shard_map/all_to_all | solution.py:53
  36.5 36.5 %copy-start.1 = (bf16[16,2048]{1,0:T(8,128)(2,1)S(1)}, bf16[16,2048]{1,0:T(8,128)(2,1)}, u32[]{:S(2)}) copy-start(bf16[16,2048]{1,0:T(8,128)(2,1)} %param.9) | copy-start | bytes 196612
  78.4 22.7 %all-to-all-start.1 = ((f32[64,1,864]{2,1,0:T(1,128)}), f32[64,1,864]{2,1,0:T(1,128)S(1)}, u32[]{:S(2)}, u32[]{:S(2)}) async-start(f32[64,1,864]{2,1,0:T(1,128)} %reshape.492), calls=%async_computation.1 | async-start | bytes 458752 | tf_op jit(solution)/shard_map/all_to_all | solution.py:87
where the time goes:
time: 104 us
  blocking collectives  32 us (31%)
  starting transfers between devices  29.7 us (29%)
  waiting for transfers between devices  18.5 us (18%)
  matrix products  10.3 us (10%)
  other arithmetic  7.53 us (7%)
  local copies, waits for them, and re-layouts  4.92 us (5%)
    all_gather x1, blocking collectives, on_device(): full = lax.all_gather(grid, 'chan', axis=0, tiled=True)  32 us
    all_to_all x1, starting transfers between devices, on_device(): lax.all_to_all(send, TILE_AXES, split_axis=1, concat_axis=1, tiled=True)  18.2 us
    all_to_all x1, starting transfers between devices, on_device(): lax.all_to_all(chunks, TILE_AXES, split_axis=0, concat_axis=0, tiled=True)  11.5 us
    all_to_all x1, waiting for transfers between devices, on_device(): lax.all_to_all(send, TILE_AXES, split_axis=1, concat_axis=1, tiled=True)  9.64 us
    all_to_all x1, waiting for transfers between devices, on_device(): lax.all_to_all(chunks, TILE_AXES, split_axis=0, concat_axis=0, tiled=True)  8.85 us
    dot_general x1, matrix products, on_device(): sums = jnp.dot(summed, member, preferred_element_type=jnp.float32)  4.43 us
    dot_general x1, matrix products, on_device(): jnp.dot(payload, select, preferred_element_type=jnp.float32)  3.06 us
    unnamed x8, local copies, waits for them, and re-layouts  2.68 us
  transfers between devices with their start and end apart: 2, of which 2 were waited for; matrix products, arithmetic and copies ran while one was open for 2% of the time, Pallas kernels for 0%

commit v1 on v0

--- a/solution.py
+++ b/solution.py
@@ -64,7 +64,10 @@
     grid = (sums[:channels] / jnp.maximum(counts, 1.0)[None, :]).astype(jnp.bfloat16)
     occupied = (counts > 0).astype(jnp.float32)
 
-    full = lax.all_gather(grid, "chan", axis=0, tiled=True)
+    chans = lax.axis_size("chan")
+    copies = jnp.broadcast_to(grid[None], (chans, *grid.shape))
+    full = lax.all_to_all(copies, "chan", split_axis=0, concat_axis=0, tiled=True)
+    full = full.reshape(chans * channels, VOX)
     masked = (grad_out.astype(jnp.float32) * occupied[None, :]).astype(jnp.bfloat16)
 
     stacked_w = weight.transpose(1, 0, 2).reshape(27 * out_rows, C_IN)

time: 104 us -> 105 us (level)
  blocking collectives: 32 us -> 0 us
  waiting for transfers between devices: 18.5 us -> 38.8 us
  starting transfers between devices: 29.7 us -> 41.3 us
    all_gather x1 -> x0, blocking collectives: 32 us -> none  [on_device(): full = lax.all_gather(grid, 'chan', axis=0, tiled=True)]
    all_to_all x0 -> x1, waiting for transfers between devices: none -> 20.4 us  [on_device(): lax.all_to_all(copies, 'chan', split_axis=0, concat_axis=0, tiled=True)]
    all_to_all x0 -> x1, starting transfers between devices: none -> 11.9 us  [on_device(): lax.all_to_all(copies, 'chan', split_axis=0, concat_axis=0, tiled=True)]
  transfers between devices with their start and end apart: 2 -> 3, of which waited for: 2 -> 3; matrix products, arithmetic and copies ran while one was open for 2% -> 5% of each run, Pallas kernels for 0% -> 0%
where the time goes in v1:
time: 105 us
  starting transfers between devices  41.3 us (39%)
  waiting for transfers between devices  38.8 us (37%)
  matrix products  10.2 us (10%)
  other arithmetic  7.53 us (7%)
  local copies, waits for them, and re-layouts  5.76 us (5%)
    all_to_all x1, waiting for transfers between devices, on_device(): lax.all_to_all(copies, 'chan', split_axis=0, concat_axis=0, tiled=True)  20.4 us
    all_to_all x1, starting transfers between devices, on_device(): lax.all_to_all(send, TILE_AXES, split_axis=1, concat_axis=1, tiled=True)  18.2 us
    all_to_all x1, starting transfers between devices, on_device(): lax.all_to_all(copies, 'chan', split_axis=0, concat_axis=0, tiled=True)  11.9 us
    all_to_all x1, starting transfers between devices, on_device(): lax.all_to_all(chunks, TILE_AXES, split_axis=0, concat_axis=0, tiled=True)  11.2 us
    all_to_all x1, waiting for transfers between devices, on_device(): lax.all_to_all(send, TILE_AXES, split_axis=1, concat_axis=1, tiled=True)  9.64 us
    all_to_all x1, waiting for transfers between devices, on_device(): lax.all_to_all(chunks, TILE_AXES, split_axis=0, concat_axis=0, tiled=True)  8.85 us
    dot_general x1, matrix products, on_device(): sums = jnp.dot(summed, member, preferred_element_type=jnp.float32)  4.43 us
    dot_general x1, matrix products, on_device(): jnp.dot(payload, select, preferred_element_type=jnp.float32)  3.06 us
  transfers between devices with their start and end apart: 3, of which 3 were waited for; matrix products, arithmetic and copies ran while one was open for 5% of the time, Pallas kernels for 0%

profile of v1, /device:TPU:1, one launch (start us, length us, event | category | flops | bytes accessed | tf_op | source)
XLA Modules:
  0.0 104.7 jit_solution(12528393926480733001)
XLA Ops:
  0.6 1.4 %fusion.7 = f32[1024]{0:T(1024)S(1)} fusion(s32[1024]{0:T(1024)} %bitcast.155), kind=kOutput, calls=%fused_computation.12 | convolution fusion | flops 135658496 | bytes 8192 | tf_op jit(solution)/shard_map/dot_general | solution.py:44
  2.0 0.7 multiply_add_fusion
  2.7 0.7 add_convert_fusion
  3.5 3.1 %fusion.5 = bf16[10,3072]{1,0:T(8,128)(2,1)S(1)} fusion(s32[1024]{0:T(1024)S(1)} %bitcast.156, bf16[1,1024]{1,0:T(2,128)(2,1)S(1)} %fusion.156, bf16[1,1024]{1,0:T(2,128)(2,1)S(1)} %get-tuple-element.2, bf16[8,1024]{1,0:T(8,128)(2,1)} %param.5), kind=kOutput, calls=%fused_computation.9 | convolution fusion | flops 66152448 | bytes 86016 | tf_op jit(solution)/shard_map/dot_general | solution.py:52
  6.5 0.2 all_to_all.12
  6.7 0.1 copy.13
  6.8 0.8 reshape.495
  7.7 18.2 %all-to-all-start = ((bf16[64,2,240]{2,1,0:T(2,128)(2,1)}), bf16[64,2,240]{2,1,0:T(2,128)(2,1)S(1)}, u32[]{:S(2)}, u32[]{:S(2)}) async-start(bf16[64,2,240]{2,1,0:T(2,128)(2,1)} %reshape.495), calls=%async_computation | async-start | bytes 131072 | tf_op jit(solution)/shard_map/all_to_all | solution.py:53
  26.1 9.6 %all-to-all-done = bf16[64,2,240]{2,1,0:T(2,128)(2,1)S(1)} async-done(((bf16[64,2,240]{2,1,0:T(2,128)(2,1)}), bf16[64,2,240]{2,1,0:T(2,128)(2,1)S(1)}, u32[]{:S(2)}, u32[]{:S(2)}) %all-to-all-start) | async-done | bytes 61472 | tf_op jit(solution)/shard_map/all_to_all | solution.py:53
  35.8 0.2 reshape.496
  36.0 0.2 fusion.120
  36.3 0.2 slice.235
  36.5 4.4 %fusion = f32[9,2048]{1,0:T(8,128)S(1)} fusion(s32[3072]{0:T(1024)S(1)} %reshape.485, bf16[8,3072]{1,0:T(8,128)(2,1)S(1)} %slice.235), kind=kOutput, calls=%fused_computation.1 | convolution fusion | flops 119537664 | bytes 135168 | tf_op jit(solution)/shard_map/dot_general | solution.py:62
  41.0 0.8 broadcast_in_dim.299
  41.8 11.9 %all-to-all-start.1 = ((bf16[16,8,2048]{2,1,0:T(8,128)(2,1)}), bf16[16,8,2048]{2,1,0:T(8,128)(2,1)S(1)}, u32[]{:S(2)}, u32[]{:S(2)}) async-start(bf16[16,8,2048]{2,1,0:T(8,128)(2,1)} %broadcast_in_dim.299), calls=%async_computation.1 | async-start | bytes 1048576 | tf_op jit(solution)/shard_map/all_to_all | solution.py:69
  54.6 0.1 fusion.73
  54.7 0.1 fusion.76
  54.8 0.1 fusion.79
  54.9 0.1 fusion.82
  56.1 20.4 %all-to-all-done.1 = bf16[16,8,2048]{2,1,0:T(8,128)(2,1)S(1)} async-done(((bf16[16,8,2048]{2,1,0:T(8,128)(2,1)}), bf16[16,8,2048]{2,1,0:T(8,128)(2,1)S(1)}, u32[]{:S(2)}, u32[]{:S(2)}) %all-to-all-start.1) | async-done | bytes 524320 | tf_op jit(solution)/shard_map/all_to_all | solution.py:69
  76.5 0.6 convolution_bitcast_fusion.1
  77.2 0.7 reshape_reshape.3
  77.9 0.3 copy.11
  78.2 1.2 %reshape.497 = f32[64,1,864]{2,1,0:T(1,128)} reshape(f32[64,16,54]{2,1,0:T(8,128)S(1)} %copy.11) | data formatting | bytes 442368
  79.5 11.2 %all-to-all-start.2 = ((f32[64,1,864]{2,1,0:T(1,128)}), f32[64,1,864]{2,1,0:T(1,128)S(1)}, u32[]{:S(2)}, u32[]{:S(2)}) async-start(f32[64,1,864]{2,1,0:T(1,128)} %reshape.497), calls=%async_computation.2 | async-start | bytes 458752 | tf_op jit(solution)/shard_map/all_to_all | solution.py:90
  90.7 0.8 convolution_bitcast_fusion
  91.5 1.6 %fusion.13 = bf16[16,2048]{1,0:T(8,128)(2,1)} fusion(f32[432,2594]{1,0:T(8,128)S(1)} %convolution_bitcast_fusion, f32[2048]{0:T(1024)S(1)} %bitcast.152, pred[2048]{0:T(1024)(128)(4,1)S(1)} %get-tuple-element.4, pred[2048]{0:T(1024)(128)(4,1)S(1)} %get-tuple-element.5, pred[2048]{0:T(1024)(128)(4,1)S(1)} %get-tuple-element.6, ...), kind=kLoop, calls=%fused_computation.20 | loop fusion | flops 1802240 | bytes 3667968 | tf_op jit(solution)/shard_map/convert_element_type | solution.py:80
  93.1 8.8 %all-to-all-done.2 = f32[64,1,864]{2,1,0:T(1,128)S(1)} async-done(((f32[64,1,864]{2,1,0:T(1,128)}), f32[64,1,864]{2,1,0:T(1,128)S(1)}, u32[]{:S(2)}, u32[]{:S(2)}) %all-to-all-start.2) | async-done | bytes 221216 | tf_op jit(solution)/shard_map/all_to_all | solution.py:90
  101.9 0.5 broadcast.2888
  102.5 1.2 %reduce.4 = f32[64,864]{1,0:T(8,128)S(1)} reduce(f32[64,1,864]{2,1,0:T(1,128)S(1)} %all-to-all-done.2, f32[]{:T(128)} %broadcast.2888), dimensions={1}, to_apply=%all_to_all.15.reduce_sub_computation | reduce | bytes 442372 | tf_op jit(solution)/shard_map/all_to_all | solution.py:90
  103.6 0.4 reshape.498
  104.1 0.7 reduce_sum.19
  (51 shorter events, 2.3 us)
Async XLA Ops:
  0.6 90.1 %copy-start = (bf16[16,27,128]{2,0,1:T(8,128)(2,1)S(1)}, bf16[16,27,128]{2,0,1:T(8,128)(2,1)}, u32[]{:S(2)}) copy-start(bf16[16,27,128]{2,0,1:T(8,128)(2,1)} %param.8) | copy-start | bytes 331780
  7.7 28.1 %all-to-all-start = ((bf16[64,2,240]{2,1,0:T(2,128)(2,1)}), bf16[64,2,240]{2,1,0:T(2,128)(2,1)S(1)}, u32[]{:S(2)}, u32[]{:S(2)}) async-start(bf16[64,2,240]{2,1,0:T(2,128)(2,1)} %reshape.495), calls=%async_computation | async-start | bytes 131072 | tf_op jit(solution)/shard_map/all_to_all | solution.py:53
  40.9 12.8 %copy-start.1 = (bf16[16,2048]{1,0:T(8,128)(2,1)S(1)}, bf16[16,2048]{1,0:T(8,128)(2,1)}, u32[]{:S(2)}) copy-start(bf16[16,2048]{1,0:T(8,128)(2,1)} %param.9) | copy-start | bytes 196612
  41.8 34.6 %all-to-all-start.1 = ((bf16[16,8,2048]{2,1,0:T(8,128)(2,1)}), bf16[16,8,2048]{2,1,0:T(8,128)(2,1)S(1)}, u32[]{:S(2)}, u32[]{:S(2)}) async-start(bf16[16,8,2048]{2,1,0:T(8,128)(2,1)} %broadcast_in_dim.299), calls=%async_computation.1 | async-start | bytes 1048576 | tf_op jit(solution)/shard_map/all_to_all | solution.py:69
  79.5 22.5 %all-to-all-start.2 = ((f32[64,1,864]{2,1,0:T(1,128)}), f32[64,1,864]{2,1,0:T(1,128)S(1)}, u32[]{:S(2)}, u32[]{:S(2)}) async-start(f32[64,1,864]{2,1,0:T(1,128)} %reshape.497), calls=%async_computation.2 | async-start | bytes 458752 | tf_op jit(solution)/shard_map/all_to_all | solution.py:90

commit v2 on v0

--- a/solution.py
+++ b/solution.py
@@ -77,15 +77,16 @@
     features_out = (output * occupied[None, :]).astype(jnp.bfloat16)
 
     wide_masked = jnp.pad(masked, ((0, 0), (REACH, REACH)))
-    moved = jnp.stack([shifted(wide_masked, k, -1) for k in range(27)]).reshape(27 * out_rows, VOX)
+    moved = jnp.stack([shifted(wide_masked, k, -1) for k in range(27)])
     grads = lax.dot_general(
-        moved, full, (((1,), (1,)), ((), ())), preferred_element_type=jnp.float32
+        moved.reshape(27 * out_rows, VOX), full, (((1,), (1,)), ((), ())),
+        preferred_element_type=jnp.float32,
     )
-    grads = grads.reshape(27, out_rows, C_IN).transpose(1, 0, 2).reshape(out_rows, 27 * C_IN)
-    width = grads.shape[1] // tiles
-    chunks = grads.reshape(out_rows, tiles, width).transpose(1, 0, 2)
+    width = 27 * C_IN // tiles
+    grads = grads.reshape(27, out_rows, C_IN).transpose(1, 0, 2).reshape(out_rows, tiles, width)
+    chunks = grads.transpose(1, 0, 2).reshape(tiles, out_rows * width)
     arrived = lax.all_to_all(chunks, TILE_AXES, split_axis=0, concat_axis=0, tiled=True)
-    weight_grad = jnp.sum(arrived, axis=0)
+    weight_grad = jnp.sum(arrived, axis=0).reshape(out_rows, width)
     return (features_out, weight_grad)
 
 

time: 104 us -> 102 us (0.981)
  other arithmetic: 7.53 us -> 5.85 us
    unnamed x8 -> x6, local copies, waits for them, and re-layouts: 2.68 us -> 1.06 us
    reshape x0 -> x2, local copies, waits for them, and re-layouts: none -> 1.43 us  [the longest x1 0.74 us: on_device(): grads.reshape(27, out_rows, C_IN).transpose(1, 0, 2)]
    all_to_all x1 -> x0, other arithmetic: 1.18 us -> none  [on_device(): lax.all_to_all(chunks, TILE_AXES, split_axis=0, concat_axis=0, tiled=True)]
  transfers between devices with their start and end apart: 2 -> 2, of which waited for: 2 -> 2; matrix products, arithmetic and copies ran while one was open for 2% -> 3% of each run, Pallas kernels for 0% -> 0%
where the time goes in v2:
time: 102 us
  blocking collectives  32 us (31%)
  starting transfers between devices  29.7 us (29%)
  waiting for transfers between devices  18.5 us (18%)
  matrix products  10.3 us (10%)
  other arithmetic  5.85 us (6%)
  local copies, waits for them, and re-layouts  4.69 us (5%)
    all_gather x1, blocking collectives, on_device(): full = lax.all_gather(grid, 'chan', axis=0, tiled=True)  32 us
    all_to_all x1, starting transfers between devices, on_device(): lax.all_to_all(send, TILE_AXES, split_axis=1, concat_axis=1, tiled=True)  18.2 us
    all_to_all x1, starting transfers between devices, on_device(): lax.all_to_all(chunks, TILE_AXES, split_axis=0, concat_axis=0, tiled=True)  11.5 us
    all_to_all x1, waiting for transfers between devices, on_device(): lax.all_to_all(send, TILE_AXES, split_axis=1, concat_axis=1, tiled=True)  9.64 us
    all_to_all x1, waiting for transfers between devices, on_device(): lax.all_to_all(chunks, TILE_AXES, split_axis=0, concat_axis=0, tiled=True)  8.85 us
    dot_general x1, matrix products, on_device(): sums = jnp.dot(summed, member, preferred_element_type=jnp.float32)  4.43 us
    dot_general x1, matrix products, on_device(): jnp.dot(payload, select, preferred_element_type=jnp.float32)  3.06 us
    unnamed x26, other arithmetic  2.13 us
  transfers between devices with their start and end apart: 2, of which 2 were waited for; matrix products, arithmetic and copies ran while one was open for 3% of the time, Pallas kernels for 0%

profile of v2, /device:TPU:1, one launch (start us, length us, event | category | flops | bytes accessed | tf_op | source)
XLA Modules:
  0.0 102.0 jit_solution(89310003491320922)
XLA Ops:
  0.6 1.4 %fusion.7 = f32[1024]{0:T(1024)S(1)} fusion(s32[1024]{0:T(1024)} %bitcast.152), kind=kOutput, calls=%fused_computation.12 | convolution fusion | flops 135658496 | bytes 8192 | tf_op jit(solution)/shard_map/dot_general | solution.py:44
  2.0 0.7 multiply_add_fusion
  2.7 0.7 add_convert_fusion
  3.5 3.1 %fusion.5 = bf16[10,3072]{1,0:T(8,128)(2,1)S(1)} fusion(s32[1024]{0:T(1024)S(1)} %bitcast.153, bf16[1,1024]{1,0:T(2,128)(2,1)S(1)} %fusion.156, bf16[1,1024]{1,0:T(2,128)(2,1)S(1)} %get-tuple-element.2, bf16[8,1024]{1,0:T(8,128)(2,1)} %param.5), kind=kOutput, calls=%fused_computation.9 | convolution fusion | flops 66152448 | bytes 86016 | tf_op jit(solution)/shard_map/dot_general | solution.py:52
  6.5 0.2 all_to_all.12
  6.7 0.1 copy.15
  6.8 0.8 reshape.502
  7.7 18.2 %all-to-all-start = ((bf16[64,2,240]{2,1,0:T(2,128)(2,1)}), bf16[64,2,240]{2,1,0:T(2,128)(2,1)S(1)}, u32[]{:S(2)}, u32[]{:S(2)}) async-start(bf16[64,2,240]{2,1,0:T(2,128)(2,1)} %reshape.502), calls=%async_computation | async-start | bytes 131072 | tf_op jit(solution)/shard_map/all_to_all | solution.py:53
  26.1 9.6 %all-to-all-done = bf16[64,2,240]{2,1,0:T(2,128)(2,1)S(1)} async-done(((bf16[64,2,240]{2,1,0:T(2,128)(2,1)}), bf16[64,2,240]{2,1,0:T(2,128)(2,1)S(1)}, u32[]{:S(2)}, u32[]{:S(2)}) %all-to-all-start) | async-done | bytes 61472 | tf_op jit(solution)/shard_map/all_to_all | solution.py:53
  35.8 0.2 reshape.503
  36.0 0.2 fusion.120
  36.3 0.2 slice.235
  36.5 4.4 %fusion = f32[9,2048]{1,0:T(8,128)S(1)} fusion(s32[3072]{0:T(1024)S(1)} %reshape.492, bf16[8,3072]{1,0:T(8,128)(2,1)S(1)} %slice.235), kind=kOutput, calls=%fused_computation.1 | convolution fusion | flops 119537664 | bytes 135168 | tf_op jit(solution)/shard_map/dot_general | solution.py:62
  41.0 32.0 %all_gather.3 = bf16[128,2048]{1,0:T(8,128)(2,1)S(1)} all-gather(bf16[8,2048]{1,0:T(8,128)(2,1)S(1)} %fusion.119), channel_id=1, replica_groups=mesh['tx'=4,'ty'=8,'tc'=2,'chan'=16] {'chan'}, dimensions={0}, use_global_device_ids=true | all-gather | bytes 557056 | tf_op jit(solution)/shard_map/all_gather | solution.py:67
  73.8 0.1 fusion.70
  73.9 0.1 fusion.73
  74.0 0.1 fusion.76
  74.1 0.1 fusion.79
  74.2 0.1 fusion.82
  74.3 0.1 fusion.85
  74.4 0.1 fusion.88
  74.5 0.1 fusion.91
  75.3 0.7 convolution_bitcast_fusion.1
  76.1 0.7 reshape.489
  76.8 0.3 copy.12
  77.2 1.2 %all_to_all.16 = f32[64,1,864]{2,1,0:T(1,128)} reshape(f32[64,16,54]{2,1,0:T(8,128)S(1)} %copy.12) | data formatting | bytes 442368 | tf_op jit(solution)/shard_map/all_to_all | solution.py:88
  78.4 11.5 %all-to-all-start.1 = ((f32[64,1,864]{2,1,0:T(1,128)}), f32[64,1,864]{2,1,0:T(1,128)S(1)}, u32[]{:S(2)}, u32[]{:S(2)}) async-start(f32[64,1,864]{2,1,0:T(1,128)} %all_to_all.16), calls=%async_computation.1 | async-start | bytes 458752 | tf_op jit(solution)/shard_map/all_to_all | solution.py:88
  89.9 0.8 convolution_bitcast_fusion
  90.6 1.6 %fusion.13 = bf16[16,2048]{1,0:T(8,128)(2,1)} fusion(f32[432,2594]{1,0:T(8,128)S(1)} %convolution_bitcast_fusion, f32[2048]{0:T(1024)S(1)} %bitcast.149, pred[2048]{0:T(1024)(128)(4,1)S(1)} %get-tuple-element.4, pred[2048]{0:T(1024)(128)(4,1)S(1)} %get-tuple-element.5, pred[2048]{0:T(1024)(128)(4,1)S(1)} %get-tuple-element.6, ...), kind=kLoop, calls=%fused_computation.20 | loop fusion | flops 1802240 | bytes 3667968 | tf_op jit(solution)/shard_map/convert_element_type | solution.py:77
  92.2 8.9 %all-to-all-done.1 = f32[64,1,864]{2,1,0:T(1,128)S(1)} async-done(((f32[64,1,864]{2,1,0:T(1,128)}), f32[64,1,864]{2,1,0:T(1,128)S(1)}, u32[]{:S(2)}, u32[]{:S(2)}) %all-to-all-start.1) | async-done | bytes 221216 | tf_op jit(solution)/shard_map/all_to_all | solution.py:88
  101.1 0.2 reduce_sum.19
  101.3 0.7 reshape.490
  (47 shorter events, 1.9 us)
Async XLA Ops:
  0.6 89.2 %copy-start = (bf16[16,27,128]{2,0,1:T(8,128)(2,1)S(1)}, bf16[16,27,128]{2,0,1:T(8,128)(2,1)}, u32[]{:S(2)}) copy-start(bf16[16,27,128]{2,0,1:T(8,128)(2,1)} %param.8) | copy-start | bytes 331780
  7.7 28.1 %all-to-all-start = ((bf16[64,2,240]{2,1,0:T(2,128)(2,1)}), bf16[64,2,240]{2,1,0:T(2,128)(2,1)S(1)}, u32[]{:S(2)}, u32[]{:S(2)}) async-start(bf16[64,2,240]{2,1,0:T(2,128)(2,1)} %reshape.502), calls=%async_computation | async-start | bytes 131072 | tf_op jit(solution)/shard_map/all_to_all | solution.py:53
  36.5 36.5 %copy-start.1 = (bf16[16,2048]{1,0:T(8,128)(2,1)S(1)}, bf16[16,2048]{1,0:T(8,128)(2,1)}, u32[]{:S(2)}) copy-start(bf16[16,2048]{1,0:T(8,128)(2,1)} %param.9) | copy-start | bytes 196612
  78.4 22.7 %all-to-all-start.1 = ((f32[64,1,864]{2,1,0:T(1,128)}), f32[64,1,864]{2,1,0:T(1,128)S(1)}, u32[]{:S(2)}, u32[]{:S(2)}) async-start(f32[64,1,864]{2,1,0:T(1,128)} %all_to_all.16), calls=%async_computation.1 | async-start | bytes 458752 | tf_op jit(solution)/shard_map/all_to_all | solution.py:88

commit v3 on v2

--- a/solution.py
+++ b/solution.py
@@ -29,6 +29,25 @@
     d = (a * EDGE + b) * EDGE + e
     part = padded[:, REACH + d : REACH + d + VOX]
     return jnp.where(valid(a, b, e), part, jnp.zeros_like(part))
+
+
+def moved_stack(masked):
+    v = lax.broadcasted_iota(jnp.int32, (1, VOX), 1)
+    coords = (v // (EDGE * EDGE), v // EDGE % EDGE, v % EDGE)
+    sizes = (DEPTH, EDGE, EDGE)
+    strides = (EDGE * EDGE, EDGE, 1)
+    stage = masked
+    for axis in (2, 1, 0):
+        step, size, where_ = strides[axis], sizes[axis], coords[axis]
+        pads = [(0, 0)] * (stage.ndim - 1) + [(step, step)]
+        wide = jnp.pad(stage, pads)
+        parts = []
+        for shift in (-1, 0, 1):
+            part = wide[..., step - shift * step : step - shift * step + VOX]
+            keep = (where_ - shift >= 0) & (where_ - shift < size)
+            parts.append(jnp.where(keep, part, jnp.zeros_like(part)))
+        stage = jnp.stack(parts)
+    return stage.reshape(27 * masked.shape[0], VOX)
 
 
 def on_device(tiles, points, dest, voxel, weight, grad_out):
@@ -76,11 +95,9 @@
         output = part if output is None else output + part
     features_out = (output * occupied[None, :]).astype(jnp.bfloat16)
 
-    wide_masked = jnp.pad(masked, ((0, 0), (REACH, REACH)))
-    moved = jnp.stack([shifted(wide_masked, k, -1) for k in range(27)])
+    moved = moved_stack(masked)
     grads = lax.dot_general(
-        moved.reshape(27 * out_rows, VOX), full, (((1,), (1,)), ((), ())),
-        preferred_element_type=jnp.float32,
+        moved, full, (((1,), (1,)), ((), ())), preferred_element_type=jnp.float32
     )
     width = 27 * C_IN // tiles
     grads = grads.reshape(27, out_rows, C_IN).transpose(1, 0, 2).reshape(out_rows, tiles, width)

time: 102 us -> 101 us (level)
  other arithmetic: 5.85 us -> 4.62 us
    unnamed x26 -> x0, other arithmetic: 2.13 us -> none
where the time goes in v3:
time: 101 us
  blocking collectives  32 us (32%)
  starting transfers between devices  29.7 us (29%)
  waiting for transfers between devices  18.4 us (18%)
  matrix products  10.2 us (10%)
  local copies, waits for them, and re-layouts  4.69 us (5%)
  other arithmetic  4.62 us (5%)
    all_gather x1, blocking collectives, on_device(): full = lax.all_gather(grid, 'chan', axis=0, tiled=True)  32 us
    all_to_all x1, starting transfers between devices, on_device(): lax.all_to_all(send, TILE_AXES, split_axis=1, concat_axis=1, tiled=True)  18.2 us
    all_to_all x1, starting transfers between devices, on_device(): lax.all_to_all(chunks, TILE_AXES, split_axis=0, concat_axis=0, tiled=True)  11.5 us
    all_to_all x1, waiting for transfers between devices, on_device(): lax.all_to_all(send, TILE_AXES, split_axis=1, concat_axis=1, tiled=True)  9.55 us
    all_to_all x1, waiting for transfers between devices, on_device(): lax.all_to_all(chunks, TILE_AXES, split_axis=0, concat_axis=0, tiled=True)  8.85 us
    dot_general x1, matrix products, on_device(): sums = jnp.dot(summed, member, preferred_element_type=jnp.float32)  4.43 us
    dot_general x1, matrix products, on_device(): jnp.dot(payload, select, preferred_element_type=jnp.float32)  3.05 us
  transfers between devices with their start and end apart: 2, of which 2 were waited for; matrix products, arithmetic and copies ran while one was open for 3% of the time, Pallas kernels for 0%

profile of v3, /device:TPU:1, one launch (start us, length us, event | category | flops | bytes accessed | tf_op | source)
XLA Modules:
  0.0 100.6 jit_solution(7999333328005113523)
XLA Ops:
  0.6 0.7 add_convert_fusion
  1.4 1.4 %fusion.8 = f32[1024]{0:T(1024)S(1)} fusion(s32[1024]{0:T(1024)} %bitcast.73), kind=kOutput, calls=%fused_computation.16 | convolution fusion | flops 135658496 | bytes 8192 | tf_op jit(solution)/shard_map/dot_general | solution.py:63
  2.8 0.7 multiply_add_fusion
  3.5 3.1 %fusion.5 = bf16[10,3072]{1,0:T(8,128)(2,1)S(1)} fusion(s32[1024]{0:T(1024)S(1)} %bitcast.74, bf16[1,1024]{1,0:T(2,128)(2,1)S(1)} %fusion.102, bf16[1,1024]{1,0:T(2,128)(2,1)S(1)} %get-tuple-element.4, bf16[8,1024]{1,0:T(8,128)(2,1)} %param.5), kind=kOutput, calls=%fused_computation.9 | convolution fusion | flops 66152448 | bytes 86016 | tf_op jit(solution)/shard_map/dot_general | solution.py:71
  6.5 0.2 all_to_all.12
  6.7 0.1 copy.15
  6.9 0.8 reshape.665
  7.7 18.2 %all-to-all-start = ((bf16[64,2,240]{2,1,0:T(2,128)(2,1)}), bf16[64,2,240]{2,1,0:T(2,128)(2,1)S(1)}, u32[]{:S(2)}, u32[]{:S(2)}) async-start(bf16[64,2,240]{2,1,0:T(2,128)(2,1)} %reshape.665), calls=%async_computation | async-start | bytes 131072 | tf_op jit(solution)/shard_map/all_to_all | solution.py:72
  26.3 9.6 %all-to-all-done = bf16[64,2,240]{2,1,0:T(2,128)(2,1)S(1)} async-done(((bf16[64,2,240]{2,1,0:T(2,128)(2,1)}), bf16[64,2,240]{2,1,0:T(2,128)(2,1)S(1)}, u32[]{:S(2)}, u32[]{:S(2)}) %all-to-all-start) | async-done | bytes 61472 | tf_op jit(solution)/shard_map/all_to_all | solution.py:72
  35.8 0.2 reshape.666
  36.0 0.2 fusion.66
  36.3 0.2 slice.177
  36.4 0.1 reshape.655
  36.5 4.4 %fusion = f32[9,2048]{1,0:T(8,128)S(1)} fusion(s32[3072]{0:T(1024)S(1)} %reshape.655, bf16[8,3072]{1,0:T(8,128)(2,1)S(1)} %slice.177), kind=kOutput, calls=%fused_computation.1 | convolution fusion | flops 119537664 | bytes 135168 | tf_op jit(solution)/shard_map/dot_general | solution.py:81
  41.0 0.1 fusion.62
  41.3 32.0 %all_gather.3 = bf16[128,2048]{1,0:T(8,128)(2,1)S(1)} all-gather(bf16[8,2048]{1,0:T(8,128)(2,1)S(1)} %fusion.59), channel_id=1, replica_groups=mesh['tx'=4,'ty'=8,'tc'=2,'chan'=16] {'chan'}, dimensions={0}, use_global_device_ids=true | all-gather | bytes 557056 | tf_op jit(solution)/shard_map/all_gather | solution.py:86
  73.3 0.1 fusion.24
  73.4 0.1 fusion.25
  73.6 0.1 fusion.16
  73.7 0.1 maximum_select_fusion
  73.8 0.2 pad_maximum_fusion
  74.0 0.6 convolution_bitcast_fusion.1
  74.6 0.1 copy.11
  74.7 0.7 reshape.652
  75.5 0.3 copy.12
  75.8 1.2 %all_to_all.16 = f32[64,1,864]{2,1,0:T(1,128)} reshape(f32[64,16,54]{2,1,0:T(8,128)S(1)} %copy.12) | data formatting | bytes 442368 | tf_op jit(solution)/shard_map/all_to_all | solution.py:105
  77.0 11.5 %all-to-all-start.1 = ((f32[64,1,864]{2,1,0:T(1,128)}), f32[64,1,864]{2,1,0:T(1,128)S(1)}, u32[]{:S(2)}, u32[]{:S(2)}) async-start(f32[64,1,864]{2,1,0:T(1,128)} %all_to_all.16), calls=%async_computation.1 | async-start | bytes 458752 | tf_op jit(solution)/shard_map/all_to_all | solution.py:105
  88.5 0.8 convolution_bitcast_fusion
  89.3 1.6 %fusion.31 = bf16[16,2048]{1,0:T(8,128)(2,1)} fusion(f32[432,2594]{1,0:T(8,128)S(1)} %convolution_bitcast_fusion, f32[2048]{0:T(1024)S(1)} %bitcast.70, pred[2048]{0:T(1024)(128)(4,1)S(1)} %get-tuple-element.21, pred[2048]{0:T(1024)(128)(4,1)S(1)} %get-tuple-element.22, pred[2048]{0:T(1024)(128)(4,1)S(1)} %get-tuple-element.23, ...), kind=kLoop, calls=%fused_computation.49 | loop fusion | flops 1802240 | bytes 3667968 | tf_op jit(solution)/shard_map/convert_element_type | solution.py:96
  90.9 8.8 %all-to-all-done.1 = f32[64,1,864]{2,1,0:T(1,128)S(1)} async-done(((f32[64,1,864]{2,1,0:T(1,128)}), f32[64,1,864]{2,1,0:T(1,128)S(1)}, u32[]{:S(2)}, u32[]{:S(2)}) %all-to-all-start.1) | async-done | bytes 221216 | tf_op jit(solution)/shard_map/all_to_all | solution.py:105
  99.7 0.2 reduce_sum.19
  99.9 0.7 reshape.653
  (35 shorter events, 0.5 us)
Async XLA Ops:
  0.6 87.8 %copy-start = (bf16[16,27,128]{2,0,1:T(8,128)(2,1)S(1)}, bf16[16,27,128]{2,0,1:T(8,128)(2,1)}, u32[]{:S(2)}) copy-start(bf16[16,27,128]{2,0,1:T(8,128)(2,1)} %param.8) | copy-start | bytes 331780
  7.7 28.1 %all-to-all-start = ((bf16[64,2,240]{2,1,0:T(2,128)(2,1)}), bf16[64,2,240]{2,1,0:T(2,128)(2,1)S(1)}, u32[]{:S(2)}, u32[]{:S(2)}) async-start(bf16[64,2,240]{2,1,0:T(2,128)(2,1)} %reshape.665), calls=%async_computation | async-start | bytes 131072 | tf_op jit(solution)/shard_map/all_to_all | solution.py:72
  36.5 4.4 %copy-start.1 = (bf16[16,2048]{1,0:T(8,128)(2,1)S(1)}, bf16[16,2048]{1,0:T(8,128)(2,1)}, u32[]{:S(2)}) copy-start(bf16[16,2048]{1,0:T(8,128)(2,1)} %param.9) | copy-start | bytes 196612
  77.0 22.7 %all-to-all-start.1 = ((f32[64,1,864]{2,1,0:T(1,128)}), f32[64,1,864]{2,1,0:T(1,128)S(1)}, u32[]{:S(2)}, u32[]{:S(2)}) async-start(f32[64,1,864]{2,1,0:T(1,128)} %all_to_all.16), calls=%async_computation.1 | async-start | bytes 458752 | tf_op jit(solution)/shard_map/all_to_all | solution.py:105

commit v4 on v3

--- a/solution.py
+++ b/solution.py
@@ -101,9 +101,10 @@
     )
     width = 27 * C_IN // tiles
     grads = grads.reshape(27, out_rows, C_IN).transpose(1, 0, 2).reshape(out_rows, tiles, width)
-    chunks = grads.transpose(1, 0, 2).reshape(tiles, out_rows * width)
+    lanes = -(-width // 128) * 128
+    chunks = jnp.pad(grads, ((0, 0), (0, 0), (0, lanes - width))).transpose(1, 0, 2)
     arrived = lax.all_to_all(chunks, TILE_AXES, split_axis=0, concat_axis=0, tiled=True)
-    weight_grad = jnp.sum(arrived, axis=0).reshape(out_rows, width)
+    weight_grad = jnp.sum(arrived, axis=0)[:, :width]
     return (features_out, weight_grad)
 
 

time: 101 us -> 107 us (1.059)
  waiting for transfers between devices: 18.4 us -> 24.5 us
  local copies, waits for them, and re-layouts: 4.69 us -> 3.62 us
    all_to_all x1, waiting for transfers between devices: 8.85 us -> 14.9 us  [on_device(): lax.all_to_all(chunks, TILE_AXES, split_axis=0, concat_axis=0, tiled=True)]
    all_to_all x1 -> x0, local copies, waits for them, and re-layouts: 1.23 us -> none  [on_device(): lax.all_to_all(chunks, TILE_AXES, split_axis=0, concat_axis=0, tiled=True)]
  transfers between devices with their start and end apart: 2 -> 2, of which waited for: 2 -> 2; matrix products, arithmetic and copies ran while one was open for 3% -> 2% of each run, Pallas kernels for 0% -> 0%
where the time goes in v4:
time: 107 us; the launch traced here: 106 us
  blocking collectives  32 us (30%)
  starting transfers between devices  29.7 us (28%)
  waiting for transfers between devices  24.5 us (23%)
  matrix products  10.2 us (10%)
  other arithmetic  5.1 us (5%)
  local copies, waits for them, and re-layouts  3.62 us (3%)
    all_gather x1, blocking collectives, on_device(): full = lax.all_gather(grid, 'chan', axis=0, tiled=True)  32 us
    all_to_all x1, starting transfers between devices, on_device(): lax.all_to_all(send, TILE_AXES, split_axis=1, concat_axis=1, tiled=True)  18.2 us
    all_to_all x1, waiting for transfers between devices, on_device(): lax.all_to_all(chunks, TILE_AXES, split_axis=0, concat_axis=0, tiled=True)  14.9 us
    all_to_all x1, starting transfers between devices, on_device(): lax.all_to_all(chunks, TILE_AXES, split_axis=0, concat_axis=0, tiled=True)  11.5 us
    all_to_all x1, waiting for transfers between devices, on_device(): lax.all_to_all(send, TILE_AXES, split_axis=1, concat_axis=1, tiled=True)  9.61 us
    dot_general x1, matrix products, on_device(): sums = jnp.dot(summed, member, preferred_element_type=jnp.float32)  4.43 us
    dot_general x1, matrix products, on_device(): jnp.dot(payload, select, preferred_element_type=jnp.float32)  3.05 us
  transfers between devices with their start and end apart: 2, of which 2 were waited for; matrix products, arithmetic and copies ran while one was open for 2% of the time, Pallas kernels for 0%

profile of v4, /device:TPU:1, one launch (start us, length us, event | category | flops | bytes accessed | tf_op | source)
XLA Modules:
  0.0 106.1 jit_solution(6977581863882485391)
XLA Ops:
  0.6 0.0 copy-start
  0.6 0.7 add_convert_fusion
  1.4 1.4 %fusion.8 = f32[1024]{0:T(1024)S(1)} fusion(s32[1024]{0:T(1024)} %bitcast.75), kind=kOutput, calls=%fused_computation.16 | convolution fusion | flops 135658496 | bytes 8192 | tf_op jit(solution)/shard_map/dot_general | solution.py:63
  2.8 0.7 multiply_add_fusion
  3.5 3.1 %fusion.5 = bf16[10,3072]{1,0:T(8,128)(2,1)S(1)} fusion(s32[1024]{0:T(1024)S(1)} %bitcast.76, bf16[1,1024]{1,0:T(2,128)(2,1)S(1)} %fusion.102, bf16[1,1024]{1,0:T(2,128)(2,1)S(1)} %get-tuple-element.4, bf16[8,1024]{1,0:T(8,128)(2,1)} %param.5), kind=kOutput, calls=%fused_computation.9 | convolution fusion | flops 66152448 | bytes 86016 | tf_op jit(solution)/shard_map/dot_general | solution.py:71
  6.5 0.2 all_to_all.9
  6.7 0.1 copy.13
  6.9 0.8 reshape.657
  7.7 18.2 %all-to-all-start = ((bf16[64,2,240]{2,1,0:T(2,128)(2,1)}), bf16[64,2,240]{2,1,0:T(2,128)(2,1)S(1)}, u32[]{:S(2)}, u32[]{:S(2)}) async-start(bf16[64,2,240]{2,1,0:T(2,128)(2,1)} %reshape.657), calls=%async_computation | async-start | bytes 131072 | tf_op jit(solution)/shard_map/all_to_all | solution.py:72
  26.2 9.6 %all-to-all-done = bf16[64,2,240]{2,1,0:T(2,128)(2,1)S(1)} async-done(((bf16[64,2,240]{2,1,0:T(2,128)(2,1)}), bf16[64,2,240]{2,1,0:T(2,128)(2,1)S(1)}, u32[]{:S(2)}, u32[]{:S(2)}) %all-to-all-start) | async-done | bytes 61472 | tf_op jit(solution)/shard_map/all_to_all | solution.py:72
  35.8 0.2 reshape.658
  36.0 0.2 fusion.66
  36.3 0.2 slice.180
  36.4 0.1 reshape.647
  36.5 4.4 %fusion = f32[9,2048]{1,0:T(8,128)S(1)} fusion(s32[3072]{0:T(1024)S(1)} %reshape.647, bf16[8,3072]{1,0:T(8,128)(2,1)S(1)} %slice.180), kind=kOutput, calls=%fused_computation.1 | convolution fusion | flops 119537664 | bytes 135168 | tf_op jit(solution)/shard_map/dot_general | solution.py:81
  41.0 0.1 fusion.62
  41.3 32.0 %all_gather.3 = bf16[128,2048]{1,0:T(8,128)(2,1)S(1)} all-gather(bf16[8,2048]{1,0:T(8,128)(2,1)S(1)} %fusion.59), channel_id=1, replica_groups=mesh['tx'=4,'ty'=8,'tc'=2,'chan'=16] {'chan'}, dimensions={0}, use_global_device_ids=true | all-gather | bytes 557056 | tf_op jit(solution)/shard_map/all_gather | solution.py:86
  73.3 0.1 fusion.24
  73.4 0.1 fusion.25
  73.5 0.1 fusion.13
  73.6 0.1 fusion.16
  73.7 0.1 maximum_select_fusion
  73.8 0.2 pad_maximum_fusion
  74.0 0.6 convolution_bitcast_fusion.1
  74.6 0.1 copy.10
  74.7 0.7 reshape.645
  75.5 1.1 %copy.11 = f32[64,16,128]{2,1,0:T(8,128)} copy(f32[64,16,128]{2,0,1:T(8,128)S(1)} %pad_bitcast_fusion) | data formatting | bytes 1048576 | tf_op jit(solution)/shard_map/transpose | solution.py:105
  76.6 11.5 %all-to-all-start.1 = ((f32[64,16,128]{2,1,0:T(8,128)}), f32[64,16,128]{2,1,0:T(8,128)S(1)}, u32[]{:S(2)}, u32[]{:S(2)}) async-start(f32[64,16,128]{2,1,0:T(8,128)} %copy.11), calls=%async_computation.1 | async-start | bytes 1048576 | tf_op jit(solution)/shard_map/all_to_all | solution.py:106
  88.2 0.8 convolution_bitcast_fusion
  89.0 1.6 %fusion.31 = bf16[16,2048]{1,0:T(8,128)(2,1)} fusion(f32[432,2594]{1,0:T(8,128)S(1)} %convolution_bitcast_fusion, f32[2048]{0:T(1024)S(1)} %bitcast.71, pred[2048]{0:T(1024)(128)(4,1)S(1)} %get-tuple-element.21, pred[2048]{0:T(1024)(128)(4,1)S(1)} %get-tuple-element.22, pred[2048]{0:T(1024)(128)(4,1)S(1)} %get-tuple-element.23, ...), kind=kLoop, calls=%fused_computation.50 | loop fusion | flops 1802240 | bytes 3667968 | tf_op jit(solution)/shard_map/convert_element_type | solution.py:96
  90.6 14.9 %all-to-all-done.1 = f32[64,16,128]{2,1,0:T(8,128)S(1)} async-done(((f32[64,16,128]{2,1,0:T(8,128)}), f32[64,16,128]{2,1,0:T(8,128)S(1)}, u32[]{:S(2)}, u32[]{:S(2)}) %all-to-all-start.1) | async-done | bytes 524320 | tf_op jit(solution)/shard_map/all_to_all | solution.py:106
  105.5 0.7 reduce_sum.19
  (34 shorter events, 0.5 us)
Async XLA Ops:
  0.6 87.5 %copy-start = (bf16[16,27,128]{2,0,1:T(8,128)(2,1)S(1)}, bf16[16,27,128]{2,0,1:T(8,128)(2,1)}, u32[]{:S(2)}) copy-start(bf16[16,27,128]{2,0,1:T(8,128)(2,1)} %param.8) | copy-start | bytes 331780
  7.7 28.1 %all-to-all-start = ((bf16[64,2,240]{2,1,0:T(2,128)(2,1)}), bf16[64,2,240]{2,1,0:T(2,128)(2,1)S(1)}, u32[]{:S(2)}, u32[]{:S(2)}) async-start(bf16[64,2,240]{2,1,0:T(2,128)(2,1)} %reshape.657), calls=%async_computation | async-start | bytes 131072 | tf_op jit(solution)/shard_map/all_to_all | solution.py:72
  36.5 4.4 %copy-start.1 = (bf16[16,2048]{1,0:T(8,128)(2,1)S(1)}, bf16[16,2048]{1,0:T(8,128)(2,1)}, u32[]{:S(2)}) copy-start(bf16[16,2048]{1,0:T(8,128)(2,1)} %param.9) | copy-start | bytes 196612
  76.6 28.8 %all-to-all-start.1 = ((f32[64,16,128]{2,1,0:T(8,128)}), f32[64,16,128]{2,1,0:T(8,128)S(1)}, u32[]{:S(2)}, u32[]{:S(2)}) async-start(f32[64,16,128]{2,1,0:T(8,128)} %copy.11), calls=%async_computation.1 | async-start | bytes 1048576 | tf_op jit(solution)/shard_map/all_to_all | solution.py:106

commit v5 on v3

--- a/solution.py
+++ b/solution.py
@@ -101,7 +101,7 @@
     )
     width = 27 * C_IN // tiles
     grads = grads.reshape(27, out_rows, C_IN).transpose(1, 0, 2).reshape(out_rows, tiles, width)
-    chunks = grads.transpose(1, 0, 2).reshape(tiles, out_rows * width)
+    chunks = grads.transpose(1, 0, 2).reshape(tiles, 8, out_rows * width // 8)
     arrived = lax.all_to_all(chunks, TILE_AXES, split_axis=0, concat_axis=0, tiled=True)
     weight_grad = jnp.sum(arrived, axis=0).reshape(out_rows, width)
     return (features_out, weight_grad)

time: 101 us -> 101 us (level)
    all_to_all x1 -> x0, local copies, waits for them, and re-layouts: 1.23 us -> none  [on_device(): lax.all_to_all(chunks, TILE_AXES, split_axis=0, concat_axis=0, tiled=True)]
where the time goes in v5:
time: 101 us
  blocking collectives  32 us (32%)
  starting transfers between devices  29.7 us (29%)
  waiting for transfers between devices  19.2 us (19%)
  matrix products  10.2 us (10%)
  other arithmetic  4.5 us (4%)
  local copies, waits for them, and re-layouts  4.3 us (4%)
    all_gather x1, blocking collectives, on_device(): full = lax.all_gather(grid, 'chan', axis=0, tiled=True)  32 us
    all_to_all x1, starting transfers between devices, on_device(): lax.all_to_all(send, TILE_AXES, split_axis=1, concat_axis=1, tiled=True)  18.2 us
    all_to_all x1, starting transfers between devices, on_device(): lax.all_to_all(chunks, TILE_AXES, split_axis=0, concat_axis=0, tiled=True)  11.5 us
    all_to_all x1, waiting for transfers between devices, on_device(): lax.all_to_all(chunks, TILE_AXES, split_axis=0, concat_axis=0, tiled=True)  9.64 us
    all_to_all x1, waiting for transfers between devices, on_device(): lax.all_to_all(send, TILE_AXES, split_axis=1, concat_axis=1, tiled=True)  9.55 us
    dot_general x1, matrix products, on_device(): sums = jnp.dot(summed, member, preferred_element_type=jnp.float32)  4.43 us
    dot_general x1, matrix products, on_device(): jnp.dot(payload, select, preferred_element_type=jnp.float32)  3.05 us
  transfers between devices with their start and end apart: 2, of which 2 were waited for; matrix products, arithmetic and copies ran while one was open for 3% of the time, Pallas kernels for 0%

profile of v5, /device:TPU:1, one launch (start us, length us, event | category | flops | bytes accessed | tf_op | source)
XLA Modules:
  0.0 100.9 jit_solution(16601656369400539732)
XLA Ops:
  0.6 0.7 add_convert_fusion
  1.4 1.4 %fusion.8 = f32[1024]{0:T(1024)S(1)} fusion(s32[1024]{0:T(1024)} %bitcast.73), kind=kOutput, calls=%fused_computation.16 | convolution fusion | flops 135658496 | bytes 8192 | tf_op jit(solution)/shard_map/dot_general | solution.py:63
  2.8 0.7 multiply_add_fusion
  3.5 3.1 %fusion.5 = bf16[10,3072]{1,0:T(8,128)(2,1)S(1)} fusion(s32[1024]{0:T(1024)S(1)} %bitcast.74, bf16[1,1024]{1,0:T(2,128)(2,1)S(1)} %fusion.102, bf16[1,1024]{1,0:T(2,128)(2,1)S(1)} %get-tuple-element.4, bf16[8,1024]{1,0:T(8,128)(2,1)} %param.5), kind=kOutput, calls=%fused_computation.9 | convolution fusion | flops 66152448 | bytes 86016 | tf_op jit(solution)/shard_map/dot_general | solution.py:71
  6.5 0.2 all_to_all.9
  6.7 0.1 copy.14
  6.9 0.8 reshape.665
  7.7 18.2 %all-to-all-start = ((bf16[64,2,240]{2,1,0:T(2,128)(2,1)}), bf16[64,2,240]{2,1,0:T(2,128)(2,1)S(1)}, u32[]{:S(2)}, u32[]{:S(2)}) async-start(bf16[64,2,240]{2,1,0:T(2,128)(2,1)} %reshape.665), calls=%async_computation | async-start | bytes 131072 | tf_op jit(solution)/shard_map/all_to_all | solution.py:72
  26.3 9.6 %all-to-all-done = bf16[64,2,240]{2,1,0:T(2,128)(2,1)S(1)} async-done(((bf16[64,2,240]{2,1,0:T(2,128)(2,1)}), bf16[64,2,240]{2,1,0:T(2,128)(2,1)S(1)}, u32[]{:S(2)}, u32[]{:S(2)}) %all-to-all-start) | async-done | bytes 61472 | tf_op jit(solution)/shard_map/all_to_all | solution.py:72
  35.8 0.2 reshape.666
  36.0 0.2 fusion.66
  36.3 0.2 slice.177
  36.4 0.1 reshape.655
  36.5 4.4 %fusion = f32[9,2048]{1,0:T(8,128)S(1)} fusion(s32[3072]{0:T(1024)S(1)} %reshape.655, bf16[8,3072]{1,0:T(8,128)(2,1)S(1)} %slice.177), kind=kOutput, calls=%fused_computation.1 | convolution fusion | flops 119537664 | bytes 135168 | tf_op jit(solution)/shard_map/dot_general | solution.py:81
  41.0 0.1 fusion.62
  41.3 32.0 %all_gather.3 = bf16[128,2048]{1,0:T(8,128)(2,1)S(1)} all-gather(bf16[8,2048]{1,0:T(8,128)(2,1)S(1)} %fusion.59), channel_id=1, replica_groups=mesh['tx'=4,'ty'=8,'tc'=2,'chan'=16] {'chan'}, dimensions={0}, use_global_device_ids=true | all-gather | bytes 557056 | tf_op jit(solution)/shard_map/all_gather | solution.py:86
  73.3 0.1 fusion.24
  73.4 0.1 fusion.25
  73.6 0.1 fusion.16
  73.7 0.1 maximum_select_fusion
  73.8 0.2 pad_maximum_fusion
  74.0 0.6 convolution_bitcast_fusion.1
  74.6 0.1 copy.11
  74.7 0.7 reshape.651
  75.5 0.3 copy.12
  75.8 0.8 reshape.652
  76.6 11.5 %all-to-all-start.1 = ((f32[64,8,108]{2,1,0:T(8,128)}), f32[64,8,108]{2,1,0:T(8,128)S(1)}, u32[]{:S(2)}, u32[]{:S(2)}) async-start(f32[64,8,108]{2,1,0:T(8,128)} %reshape.652), calls=%async_computation.1 | async-start | bytes 524288 | tf_op jit(solution)/shard_map/all_to_all | solution.py:105
  88.1 0.8 convolution_bitcast_fusion
  88.9 1.6 %fusion.31 = bf16[16,2048]{1,0:T(8,128)(2,1)} fusion(f32[432,2594]{1,0:T(8,128)S(1)} %convolution_bitcast_fusion, f32[2048]{0:T(1024)S(1)} %bitcast.70, pred[2048]{0:T(1024)(128)(4,1)S(1)} %get-tuple-element.21, pred[2048]{0:T(1024)(128)(4,1)S(1)} %get-tuple-element.22, pred[2048]{0:T(1024)(128)(4,1)S(1)} %get-tuple-element.23, ...), kind=kLoop, calls=%fused_computation.49 | loop fusion | flops 1802240 | bytes 3667968 | tf_op jit(solution)/shard_map/convert_element_type | solution.py:96
  90.5 9.6 %all-to-all-done.1 = f32[64,8,108]{2,1,0:T(8,128)S(1)} async-done(((f32[64,8,108]{2,1,0:T(8,128)}), f32[64,8,108]{2,1,0:T(8,128)S(1)}, u32[]{:S(2)}, u32[]{:S(2)}) %all-to-all-start.1) | async-done | bytes 221216 | tf_op jit(solution)/shard_map/all_to_all | solution.py:105
  100.1 0.1 reduce_sum.19
  100.2 0.7 reshape.653
  (35 shorter events, 0.5 us)
Async XLA Ops:
  0.6 87.5 %copy-start = (bf16[16,27,128]{2,0,1:T(8,128)(2,1)S(1)}, bf16[16,27,128]{2,0,1:T(8,128)(2,1)}, u32[]{:S(2)}) copy-start(bf16[16,27,128]{2,0,1:T(8,128)(2,1)} %param.8) | copy-start | bytes 331780
  7.7 28.1 %all-to-all-start = ((bf16[64,2,240]{2,1,0:T(2,128)(2,1)}), bf16[64,2,240]{2,1,0:T(2,128)(2,1)S(1)}, u32[]{:S(2)}, u32[]{:S(2)}) async-start(bf16[64,2,240]{2,1,0:T(2,128)(2,1)} %reshape.665), calls=%async_computation | async-start | bytes 131072 | tf_op jit(solution)/shard_map/all_to_all | solution.py:72
  36.5 4.4 %copy-start.1 = (bf16[16,2048]{1,0:T(8,128)(2,1)S(1)}, bf16[16,2048]{1,0:T(8,128)(2,1)}, u32[]{:S(2)}) copy-start(bf16[16,2048]{1,0:T(8,128)(2,1)} %param.9) | copy-start | bytes 196612
  76.6 23.5 %all-to-all-start.1 = ((f32[64,8,108]{2,1,0:T(8,128)}), f32[64,8,108]{2,1,0:T(8,128)S(1)}, u32[]{:S(2)}, u32[]{:S(2)}) async-start(f32[64,8,108]{2,1,0:T(8,128)} %reshape.652), calls=%async_computation.1 | async-start | bytes 524288 | tf_op jit(solution)/shard_map/all_to_all | solution.py:105

commit v6 on v5

--- a/solution.py
+++ b/solution.py
@@ -58,9 +58,17 @@
     channels = points.shape[0]
 
     onehot = (dest == jnp.arange(tiles, dtype=jnp.int32)[None, :]).astype(jnp.bfloat16)
-    rows = jnp.arange(count, dtype=jnp.int32)
+    block = 128 if count % 128 == 0 else count
+    blocks = count // block
+    rows = jnp.arange(block, dtype=jnp.int32)
     earlier = (rows[:, None] > rows[None, :]).astype(jnp.bfloat16)
-    before = jnp.dot(earlier, onehot, preferred_element_type=jnp.float32)
+    grouped = onehot.reshape(blocks, block, tiles)
+    within = jnp.einsum("ij,bjt->bit", earlier, grouped, preferred_element_type=jnp.float32)
+    ahead = jnp.arange(blocks, dtype=jnp.int32)
+    prior = (ahead[:, None] > ahead[None, :]).astype(jnp.float32)
+    totals = jnp.sum(grouped.astype(jnp.float32), axis=1)
+    offset = jnp.dot(prior, totals, precision=lax.Precision.HIGHEST)
+    before = (within + offset[:, None, :]).reshape(count, tiles)
     rank = jnp.sum(before * onehot.astype(jnp.float32), axis=1).astype(jnp.int32)
     place = dest[:, 0] * capacity + rank
 

time: 101 us -> 102 us (level)
  no operation moved by 1% of the time
where the time goes in v6:
time: 102 us; the launch traced here: 101 us
  blocking collectives  32 us (31%)
  starting transfers between devices  29.7 us (29%)
  waiting for transfers between devices  19.2 us (19%)
  matrix products  9.98 us (10%)
  other arithmetic  5.33 us (5%)
  local copies, waits for them, and re-layouts  4.29 us (4%)
    all_gather x1, blocking collectives, on_device(): full = lax.all_gather(grid, 'chan', axis=0, tiled=True)  32 us
    all_to_all x1, starting transfers between devices, on_device(): lax.all_to_all(send, TILE_AXES, split_axis=1, concat_axis=1, tiled=True)  18.2 us
    all_to_all x1, starting transfers between devices, on_device(): lax.all_to_all(chunks, TILE_AXES, split_axis=0, concat_axis=0, tiled=True)  11.5 us
    all_to_all x1, waiting for transfers between devices, on_device(): lax.all_to_all(chunks, TILE_AXES, split_axis=0, concat_axis=0, tiled=True)  9.64 us
    all_to_all x1, waiting for transfers between devices, on_device(): lax.all_to_all(send, TILE_AXES, split_axis=1, concat_axis=1, tiled=True)  9.55 us
    dot_general x1, matrix products, on_device(): sums = jnp.dot(summed, member, preferred_element_type=jnp.float32)  4.43 us
    dot_general x1, matrix products, on_device(): jnp.dot(payload, select, preferred_element_type=jnp.float32)  3.06 us
  transfers between devices with their start and end apart: 2, of which 2 were waited for; matrix products, arithmetic and copies ran while one was open for 3% of the time, Pallas kernels for 0%

profile of v6, /device:TPU:1, one launch (start us, length us, event | category | flops | bytes accessed | tf_op | source)
XLA Modules:
  0.0 101.4 jit_solution(5953857837767098406)
XLA Ops:
  0.6 0.9 convert_reduce_fusion
  1.5 0.1 fusion.111
  1.6 1.0 fusion.8
  2.6 0.7 multiply_add_fusion
  3.3 0.7 add_convert_fusion
  4.1 3.1 %fusion.4 = bf16[10,3072]{1,0:T(8,128)(2,1)S(1)} fusion(s32[1024]{0:T(1024)S(1)} %bitcast.85, bf16[1,1024]{1,0:T(2,128)(2,1)S(1)} %fusion.104, bf16[1,1024]{1,0:T(2,128)(2,1)S(1)} %get-tuple-element.4, bf16[8,1024]{1,0:T(8,128)(2,1)} %param.5), kind=kOutput, calls=%fused_computation.7 | convolution fusion | flops 66152448 | bytes 86016 | tf_op jit(solution)/shard_map/dot_general | solution.py:79
  7.1 0.2 all_to_all.9
  7.3 0.1 copy.14
  7.4 0.8 reshape.698
  8.3 18.2 %all-to-all-start = ((bf16[64,2,240]{2,1,0:T(2,128)(2,1)}), bf16[64,2,240]{2,1,0:T(2,128)(2,1)S(1)}, u32[]{:S(2)}, u32[]{:S(2)}) async-start(bf16[64,2,240]{2,1,0:T(2,128)(2,1)} %reshape.698), calls=%async_computation | async-start | bytes 131072 | tf_op jit(solution)/shard_map/all_to_all | solution.py:80
  26.8 9.6 %all-to-all-done = bf16[64,2,240]{2,1,0:T(2,128)(2,1)S(1)} async-done(((bf16[64,2,240]{2,1,0:T(2,128)(2,1)}), bf16[64,2,240]{2,1,0:T(2,128)(2,1)S(1)}, u32[]{:S(2)}, u32[]{:S(2)}) %all-to-all-start) | async-done | bytes 61472 | tf_op jit(solution)/shard_map/all_to_all | solution.py:80
  36.4 0.2 reshape.699
  36.6 0.2 fusion.68
  36.8 0.2 slice.177
  37.1 4.4 %fusion = f32[9,2048]{1,0:T(8,128)S(1)} fusion(s32[3072]{0:T(1024)S(1)} %reshape.687, bf16[8,3072]{1,0:T(8,128)(2,1)S(1)} %slice.177), kind=kOutput, calls=%fused_computation.1 | convolution fusion | flops 119537664 | bytes 135168 | tf_op jit(solution)/shard_map/dot_general | solution.py:89
  41.6 0.1 fusion.64
  41.9 32.0 %all_gather.3 = bf16[128,2048]{1,0:T(8,128)(2,1)S(1)} all-gather(bf16[8,2048]{1,0:T(8,128)(2,1)S(1)} %fusion.59), channel_id=1, replica_groups=mesh['tx'=4,'ty'=8,'tc'=2,'chan'=16] {'chan'}, dimensions={0}, use_global_device_ids=true | all-gather | bytes 557056 | tf_op jit(solution)/shard_map/all_gather | solution.py:94
  73.9 0.1 fusion.24
  74.0 0.1 fusion.25
  74.2 0.1 fusion.16
  74.3 0.1 maximum_select_fusion
  74.4 0.2 pad_maximum_fusion
  74.6 0.6 convolution_bitcast_fusion.1
  75.2 0.1 copy.11
  75.3 0.7 reshape.683
  76.0 0.3 copy.12
  76.4 0.8 reshape.684
  77.2 11.5 %all-to-all-start.1 = ((f32[64,8,108]{2,1,0:T(8,128)}), f32[64,8,108]{2,1,0:T(8,128)S(1)}, u32[]{:S(2)}, u32[]{:S(2)}) async-start(f32[64,8,108]{2,1,0:T(8,128)} %reshape.684), calls=%async_computation.1 | async-start | bytes 524288 | tf_op jit(solution)/shard_map/all_to_all | solution.py:113
  88.7 0.8 convolution_bitcast_fusion
  89.4 1.6 %fusion.31 = bf16[16,2048]{1,0:T(8,128)(2,1)} fusion(f32[432,2594]{1,0:T(8,128)S(1)} %convolution_bitcast_fusion, f32[2048]{0:T(1024)S(1)} %bitcast.80, pred[2048]{0:T(1024)(128)(4,1)S(1)} %get-tuple-element.21, pred[2048]{0:T(1024)(128)(4,1)S(1)} %get-tuple-element.22, pred[2048]{0:T(1024)(128)(4,1)S(1)} %get-tuple-element.23, ...), kind=kLoop, calls=%fused_computation.50 | loop fusion | flops 1802240 | bytes 3667968 | tf_op jit(solution)/shard_map/convert_element_type | solution.py:104
  91.0 9.6 %all-to-all-done.1 = f32[64,8,108]{2,1,0:T(8,128)S(1)} async-done(((f32[64,8,108]{2,1,0:T(8,128)}), f32[64,8,108]{2,1,0:T(8,128)S(1)}, u32[]{:S(2)}, u32[]{:S(2)}) %all-to-all-start.1) | async-done | bytes 221216 | tf_op jit(solution)/shard_map/all_to_all | solution.py:113
  100.8 0.7 reshape.685
  (37 shorter events, 0.6 us)
Async XLA Ops:
  0.6 88.0 %copy-start = (bf16[16,27,128]{2,0,1:T(8,128)(2,1)S(1)}, bf16[16,27,128]{2,0,1:T(8,128)(2,1)}, u32[]{:S(2)}) copy-start(bf16[16,27,128]{2,0,1:T(8,128)(2,1)} %param.8) | copy-start | bytes 331780
  8.3 28.1 %all-to-all-start = ((bf16[64,2,240]{2,1,0:T(2,128)(2,1)}), bf16[64,2,240]{2,1,0:T(2,128)(2,1)S(1)}, u32[]{:S(2)}, u32[]{:S(2)}) async-start(bf16[64,2,240]{2,1,0:T(2,128)(2,1)} %reshape.698), calls=%async_computation | async-start | bytes 131072 | tf_op jit(solution)/shard_map/all_to_all | solution.py:80
  37.1 4.4 %copy-start.1 = (bf16[16,2048]{1,0:T(8,128)(2,1)S(1)}, bf16[16,2048]{1,0:T(8,128)(2,1)}, u32[]{:S(2)}) copy-start(bf16[16,2048]{1,0:T(8,128)(2,1)} %param.9) | copy-start | bytes 196612
  77.2 23.5 %all-to-all-start.1 = ((f32[64,8,108]{2,1,0:T(8,128)}), f32[64,8,108]{2,1,0:T(8,128)S(1)}, u32[]{:S(2)}, u32[]{:S(2)}) async-start(f32[64,8,108]{2,1,0:T(8,128)} %reshape.684), calls=%async_computation.1 | async-start | bytes 524288 | tf_op jit(solution)/shard_map/all_to_all | solution.py:113

commit v7 on v5

--- a/solution.py
+++ b/solution.py
@@ -73,12 +73,14 @@
 
     high = received[channels].astype(jnp.int32)
     low = received[channels + 1].astype(jnp.int32)
-    cell = jnp.where(high > 0, (high - 1) * 64 + low, VOX)
-    member = (cell[:, None] == jnp.arange(VOX, dtype=jnp.int32)[None, :]).astype(jnp.bfloat16)
+    upper = (high[:, None] - 1 == jnp.arange(VOX // 64, dtype=jnp.int32)[None, :]).astype(jnp.bfloat16)
+    lower = low[None, :] == jnp.arange(64, dtype=jnp.int32)[:, None]
     summed = jnp.concatenate(
         [received[:channels], jnp.ones((1, slots), jnp.bfloat16)], axis=0
     )
-    sums = jnp.dot(summed, member, preferred_element_type=jnp.float32)
+    spread = jnp.where(lower[None], summed[:, None, :], jnp.zeros((), jnp.bfloat16))
+    split = jnp.dot(spread.reshape((channels + 1) * 64, slots), upper, preferred_element_type=jnp.float32)
+    sums = split.reshape(channels + 1, 64, VOX // 64).transpose(0, 2, 1).reshape(channels + 1, VOX)
     counts = sums[channels]
     grid = (sums[:channels] / jnp.maximum(counts, 1.0)[None, :]).astype(jnp.bfloat16)
     occupied = (counts > 0).astype(jnp.float32)

time: 101 us -> 98.8 us (0.978)
  matrix products: 10.2 us -> 7.39 us
    dot_general x1, matrix products: 4.43 us -> 1.59 us  [on_device(): jnp.dot(spread.reshape((channels + 1) * 64, slots), upper, preferred_elem...]
where the time goes in v7:
time: 98.8 us; the launch traced here: 98.4 us
  blocking collectives  31.8 us (32%)
  starting transfers between devices  29.7 us (30%)
  waiting for transfers between devices  19.2 us (19%)
  matrix products  7.39 us (7%)
  other arithmetic  4.66 us (5%)
  local copies, waits for them, and re-layouts  4.62 us (5%)
  between operations  1.01 us (1%)
    all_gather x1, blocking collectives, on_device(): full = lax.all_gather(grid, 'chan', axis=0, tiled=True)  31.8 us
    all_to_all x1, starting transfers between devices, on_device(): lax.all_to_all(send, TILE_AXES, split_axis=1, concat_axis=1, tiled=True)  18.2 us
    all_to_all x1, starting transfers between devices, on_device(): lax.all_to_all(chunks, TILE_AXES, split_axis=0, concat_axis=0, tiled=True)  11.5 us
    all_to_all x1, waiting for transfers between devices, on_device(): lax.all_to_all(chunks, TILE_AXES, split_axis=0, concat_axis=0, tiled=True)  9.64 us
    all_to_all x1, waiting for transfers between devices, on_device(): lax.all_to_all(send, TILE_AXES, split_axis=1, concat_axis=1, tiled=True)  9.55 us
    dot_general x1, matrix products, on_device(): jnp.dot(payload, select, preferred_element_type=jnp.float32)  3.05 us
  transfers between devices with their start and end apart: 2, of which 2 were waited for; matrix products, arithmetic and copies ran while one was open for 3% of the time, Pallas kernels for 0%

profile of v7, /device:TPU:1, one launch (start us, length us, event | category | flops | bytes accessed | tf_op | source)
XLA Modules:
  0.0 98.4 jit_solution(12084864741827978656)
XLA Ops:
  0.6 0.7 add_convert_fusion
  1.4 1.4 %fusion.14 = f32[1024]{0:T(1024)S(1)} fusion(s32[1024]{0:T(1024)} %bitcast.73), kind=kOutput, calls=%fused_computation.19 | convolution fusion | flops 135658496 | bytes 8192 | tf_op jit(solution)/shard_map/dot_general | solution.py:63
  2.8 0.7 multiply_add_fusion
  3.5 3.1 %fusion.6 = bf16[10,3072]{1,0:T(8,128)(2,1)S(1)} fusion(s32[1024]{0:T(1024)S(1)} %bitcast.74, bf16[1,1024]{1,0:T(2,128)(2,1)S(1)} %fusion.110, bf16[1,1024]{1,0:T(2,128)(2,1)S(1)} %get-tuple-element.6, bf16[8,1024]{1,0:T(8,128)(2,1)} %param.5), kind=kOutput, calls=%fused_computation.9 | convolution fusion | flops 66152448 | bytes 86016 | tf_op jit(solution)/shard_map/dot_general | solution.py:71
  6.5 0.2 all_to_all.9
  6.7 0.1 copy.14
  6.9 0.8 reshape.708
  7.7 18.2 %all-to-all-start = ((bf16[64,2,240]{2,1,0:T(2,128)(2,1)}), bf16[64,2,240]{2,1,0:T(2,128)(2,1)S(1)}, u32[]{:S(2)}, u32[]{:S(2)}) async-start(bf16[64,2,240]{2,1,0:T(2,128)(2,1)} %reshape.708), calls=%async_computation | async-start | bytes 131072 | tf_op jit(solution)/shard_map/all_to_all | solution.py:72
  26.3 9.6 %all-to-all-done = bf16[64,2,240]{2,1,0:T(2,128)(2,1)S(1)} async-done(((bf16[64,2,240]{2,1,0:T(2,128)(2,1)}), bf16[64,2,240]{2,1,0:T(2,128)(2,1)S(1)}, u32[]{:S(2)}, u32[]{:S(2)}) %all-to-all-start) | async-done | bytes 61472 | tf_op jit(solution)/shard_map/all_to_all | solution.py:72
  35.8 0.2 reshape.709
  36.0 0.2 fusion.74
  36.3 0.1 iota_compare_fusion.12
  36.6 0.2 slice.182
  36.8 1.6 %fusion.11 = f32[9,32,64]{2,1,0:T(8,128)S(1)} fusion(pred[64,3072]{1,0:T(8,128)(4,1)S(1)} %iota_compare_fusion.12, bf16[9,3072]{1,0:T(8,128)(2,1)S(1)} %concatenate.28, s32[3072]{0:T(1024)S(1)} %sub.262), kind=kOutput, calls=%fused_computation.18 | convolution fusion | flops 115113984 | bytes 337920 | tf_op jit(solution)/shard_map/dot_general | solution.py:82
  38.5 0.1 fusion.69
  38.8 0.1 slice.185
  39.0 31.8 %all_gather.3 = bf16[128,2048]{1,0:T(8,128)(2,1)S(1)} all-gather(bf16[8,2048]{1,0:T(8,128)(2,1)S(1)} %divide_convert_fusion), channel_id=1, replica_groups=mesh['tx'=4,'ty'=8,'tc'=2,'chan'=16] {'chan'}, dimensions={0}, use_global_device_ids=true | all-gather | bytes 557056 | tf_op jit(solution)/shard_map/all_gather | solution.py:88
  70.8 0.1 fusion.32
  70.9 0.1 fusion.34
  71.1 0.1 fusion.22
  71.2 0.1 maximum_select_fusion
  71.3 0.2 pad_maximum_fusion
  71.5 0.6 convolution_bitcast_fusion.1
  72.1 0.1 copy.11
  72.2 0.7 reshape.689
  73.0 0.3 copy.12
  73.3 0.8 reshape.690
  74.1 11.5 %all-to-all-start.1 = ((f32[64,8,108]{2,1,0:T(8,128)}), f32[64,8,108]{2,1,0:T(8,128)S(1)}, u32[]{:S(2)}, u32[]{:S(2)}) async-start(f32[64,8,108]{2,1,0:T(8,128)} %reshape.690), calls=%async_computation.1 | async-start | bytes 524288 | tf_op jit(solution)/shard_map/all_to_all | solution.py:107
  85.6 0.8 convolution_bitcast_fusion
  86.4 1.6 %fusion.40 = bf16[16,2048]{1,0:T(8,128)(2,1)} fusion(f32[432,2594]{1,0:T(8,128)S(1)} %convolution_bitcast_fusion, f32[2048]{0:T(1024)S(1)} %reshape.693, pred[2048]{0:T(1024)(128)(4,1)S(1)} %get-tuple-element.23, pred[2048]{0:T(1024)(128)(4,1)S(1)} %get-tuple-element.24, pred[2048]{0:T(1024)(128)(4,1)S(1)} %get-tuple-element.25, ...), kind=kLoop, calls=%fused_computation.56 | loop fusion | flops 1802240 | bytes 3667968 | tf_op jit(solution)/shard_map/convert_element_type | solution.py:98
  88.0 9.6 %all-to-all-done.1 = f32[64,8,108]{2,1,0:T(8,128)S(1)} async-done(((f32[64,8,108]{2,1,0:T(8,128)}), f32[64,8,108]{2,1,0:T(8,128)S(1)}, u32[]{:S(2)}, u32[]{:S(2)}) %all-to-all-start.1) | async-done | bytes 221216 | tf_op jit(solution)/shard_map/all_to_all | solution.py:107
  97.7 0.7 reshape.691
  (42 shorter events, 0.9 us)
Async XLA Ops:
  0.6 84.9 %copy-start = (bf16[16,27,128]{2,0,1:T(8,128)(2,1)S(1)}, bf16[16,27,128]{2,0,1:T(8,128)(2,1)}, u32[]{:S(2)}) copy-start(bf16[16,27,128]{2,0,1:T(8,128)(2,1)} %param.8) | copy-start | bytes 331780
  7.7 28.1 %all-to-all-start = ((bf16[64,2,240]{2,1,0:T(2,128)(2,1)}), bf16[64,2,240]{2,1,0:T(2,128)(2,1)S(1)}, u32[]{:S(2)}, u32[]{:S(2)}) async-start(bf16[64,2,240]{2,1,0:T(2,128)(2,1)} %reshape.708), calls=%async_computation | async-start | bytes 131072 | tf_op jit(solution)/shard_map/all_to_all | solution.py:72
  36.8 1.7 %copy-start.1 = (bf16[16,2048]{1,0:T(8,128)(2,1)S(1)}, bf16[16,2048]{1,0:T(8,128)(2,1)}, u32[]{:S(2)}) copy-start(bf16[16,2048]{1,0:T(8,128)(2,1)} %param.9) | copy-start | bytes 196612
  74.1 23.5 %all-to-all-start.1 = ((f32[64,8,108]{2,1,0:T(8,128)}), f32[64,8,108]{2,1,0:T(8,128)S(1)}, u32[]{:S(2)}, u32[]{:S(2)}) async-start(f32[64,8,108]{2,1,0:T(8,128)} %reshape.690), calls=%async_computation.1 | async-start | bytes 524288 | tf_op jit(solution)/shard_map/all_to_all | solution.py:107

commit v8 on v7

--- a/solution.py
+++ b/solution.py
@@ -67,8 +67,11 @@
     vox = voxel[:, 0]
     codes = jnp.stack([vox // 64 + 1, vox % 64]).astype(jnp.bfloat16)
     payload = jnp.concatenate([points, codes], axis=0)
-    select = (place[:, None] == jnp.arange(slots, dtype=jnp.int32)[None, :]).astype(jnp.bfloat16)
-    send = jnp.dot(payload, select, preferred_element_type=jnp.float32).astype(jnp.bfloat16)
+    rows_in = payload.shape[0]
+    ranked = rank[None, :] == jnp.arange(capacity, dtype=jnp.int32)[:, None]
+    spread_in = jnp.where(ranked[None], payload[:, None, :], jnp.zeros((), jnp.bfloat16))
+    packed = jnp.dot(spread_in.reshape(rows_in * capacity, count), onehot, preferred_element_type=jnp.float32)
+    send = packed.astype(jnp.bfloat16).reshape(rows_in, capacity, tiles).transpose(0, 2, 1).reshape(rows_in, slots)
     received = lax.all_to_all(send, TILE_AXES, split_axis=1, concat_axis=1, tiled=True)
 
     high = received[channels].astype(jnp.int32)

time: 98.8 us -> 95.7 us (0.969)
  matrix products: 7.39 us -> 4.76 us
    dot_general x1, matrix products: 3.05 us -> 0.41 us  [on_device(): jnp.dot(spread_in.reshape(rows_in * capacity, count), onehot, preferred_e...]
where the time goes in v8:
time: 95.7 us; the launch traced here: 95.3 us
  blocking collectives  31.8 us (33%)
  starting transfers between devices  29.7 us (31%)
  waiting for transfers between devices  19.2 us (20%)
  matrix products  4.76 us (5%)
  local copies, waits for them, and re-layouts  4.75 us (5%)
  other arithmetic  4.1 us (4%)
  between operations  1.06 us (1%)
    all_gather x1, blocking collectives, on_device(): full = lax.all_gather(grid, 'chan', axis=0, tiled=True)  31.8 us
    all_to_all x1, starting transfers between devices, on_device(): lax.all_to_all(send, TILE_AXES, split_axis=1, concat_axis=1, tiled=True)  18.2 us
    all_to_all x1, starting transfers between devices, on_device(): lax.all_to_all(chunks, TILE_AXES, split_axis=0, concat_axis=0, tiled=True)  11.5 us
    all_to_all x1, waiting for transfers between devices, on_device(): lax.all_to_all(chunks, TILE_AXES, split_axis=0, concat_axis=0, tiled=True)  9.64 us
    all_to_all x1, waiting for transfers between devices, on_device(): lax.all_to_all(send, TILE_AXES, split_axis=1, concat_axis=1, tiled=True)  9.55 us
  transfers between devices with their start and end apart: 2, of which 2 were waited for; matrix products, arithmetic and copies ran while one was open for 3% of the time, Pallas kernels for 0%

profile of v8, /device:TPU:1, one launch (start us, length us, event | category | flops | bytes accessed | tf_op | source)
XLA Modules:
  0.0 95.3 jit_solution(11253748281615619536)
XLA Ops:
  0.7 0.8 add_convert_fusion
  1.4 1.4 %fusion.11 = f32[1024]{0:T(1024)S(1)} fusion(s32[1024]{0:T(1024)} %bitcast.75), kind=kOutput, calls=%fused_computation.15 | convolution fusion | flops 135658496 | bytes 8192 | tf_op jit(solution)/shard_map/dot_general | solution.py:63
  2.9 0.1 broadcast_select_fusion
  3.0 0.4 convolution_convert_fusion
  3.4 0.1 copy.13
  3.6 0.3 copy.14
  3.8 0.8 reshape.735
  4.7 18.2 %all-to-all-start = ((bf16[64,2,240]{2,1,0:T(2,128)(2,1)}), bf16[64,2,240]{2,1,0:T(2,128)(2,1)S(1)}, u32[]{:S(2)}, u32[]{:S(2)}) async-start(bf16[64,2,240]{2,1,0:T(2,128)(2,1)} %reshape.735), calls=%async_computation | async-start | bytes 131072 | tf_op jit(solution)/shard_map/all_to_all | solution.py:75
  23.2 9.6 %all-to-all-done = bf16[64,2,240]{2,1,0:T(2,128)(2,1)S(1)} async-done(((bf16[64,2,240]{2,1,0:T(2,128)(2,1)}), bf16[64,2,240]{2,1,0:T(2,128)(2,1)S(1)}, u32[]{:S(2)}, u32[]{:S(2)}) %all-to-all-start) | async-done | bytes 61472 | tf_op jit(solution)/shard_map/all_to_all | solution.py:75
  32.8 0.2 reshape.736
  33.0 0.2 fusion.72
  33.3 0.1 iota_compare_fusion.8
  33.5 0.2 slice.182
  33.8 1.6 %fusion.8 = f32[9,32,64]{2,1,0:T(8,128)S(1)} fusion(pred[64,3072]{1,0:T(8,128)(4,1)S(1)} %iota_compare_fusion.8, bf16[9,3072]{1,0:T(8,128)(2,1)S(1)} %concatenate.28, s32[3072]{0:T(1024)S(1)} %sub.262), kind=kOutput, calls=%fused_computation.14 | convolution fusion | flops 115113984 | bytes 337920 | tf_op jit(solution)/shard_map/dot_general | solution.py:85
  35.5 0.1 fusion.67
  35.7 0.1 slice.185
  35.9 31.8 %all_gather.3 = bf16[128,2048]{1,0:T(8,128)(2,1)S(1)} all-gather(bf16[8,2048]{1,0:T(8,128)(2,1)S(1)} %divide_convert_fusion), channel_id=1, replica_groups=mesh['tx'=4,'ty'=8,'tc'=2,'chan'=16] {'chan'}, dimensions={0}, use_global_device_ids=true | all-gather | bytes 557056 | tf_op jit(solution)/shard_map/all_gather | solution.py:91
  67.8 0.1 fusion.29
  67.9 0.1 fusion.31
  68.1 0.1 fusion.19
  68.2 0.1 maximum_select_fusion
  68.3 0.2 pad_maximum_fusion
  68.5 0.6 convolution_bitcast_fusion.1
  69.1 0.1 copy.16
  69.2 0.7 reshape.716
  69.9 0.3 copy.17
  70.3 0.8 reshape.717
  71.1 11.5 %all-to-all-start.1 = ((f32[64,8,108]{2,1,0:T(8,128)}), f32[64,8,108]{2,1,0:T(8,128)S(1)}, u32[]{:S(2)}, u32[]{:S(2)}) async-start(f32[64,8,108]{2,1,0:T(8,128)} %reshape.717), calls=%async_computation.1 | async-start | bytes 524288 | tf_op jit(solution)/shard_map/all_to_all | solution.py:110
  82.6 0.8 convolution_bitcast_fusion
  83.3 1.6 %fusion.37 = bf16[16,2048]{1,0:T(8,128)(2,1)} fusion(f32[432,2594]{1,0:T(8,128)S(1)} %convolution_bitcast_fusion, f32[2048]{0:T(1024)S(1)} %reshape.720, pred[2048]{0:T(1024)(128)(4,1)S(1)} %get-tuple-element.23, pred[2048]{0:T(1024)(128)(4,1)S(1)} %get-tuple-element.24, pred[2048]{0:T(1024)(128)(4,1)S(1)} %get-tuple-element.25, ...), kind=kLoop, calls=%fused_computation.55 | loop fusion | flops 1802240 | bytes 3667968 | tf_op jit(solution)/shard_map/convert_element_type | solution.py:101
  85.0 9.6 %all-to-all-done.1 = f32[64,8,108]{2,1,0:T(8,128)S(1)} async-done(((f32[64,8,108]{2,1,0:T(8,128)}), f32[64,8,108]{2,1,0:T(8,128)S(1)}, u32[]{:S(2)}, u32[]{:S(2)}) %all-to-all-start.1) | async-done | bytes 221216 | tf_op jit(solution)/shard_map/all_to_all | solution.py:110
  94.7 0.7 reshape.718
  (48 shorter events, 0.9 us)
Async XLA Ops:
  0.6 81.9 %copy-start = (bf16[16,27,128]{2,0,1:T(8,128)(2,1)S(1)}, bf16[16,27,128]{2,0,1:T(8,128)(2,1)}, u32[]{:S(2)}) copy-start(bf16[16,27,128]{2,0,1:T(8,128)(2,1)} %param.8) | copy-start | bytes 331780
  0.6 2.3 %copy-start.3 = (s32[1024,1]{0,1:T(1,128)S(1)}, s32[1024,1]{0,1:T(1,128)}, u32[]{:S(2)}) copy-start(s32[1024,1]{0,1:T(1,128)} %param.6) | copy-start | bytes 12292
  0.7 2.2 %copy-start.2 = (bf16[8,1024]{1,0:T(8,128)(2,1)S(1)}, bf16[8,1024]{1,0:T(8,128)(2,1)}, u32[]{:S(2)}) copy-start(bf16[8,1024]{1,0:T(8,128)(2,1)} %param.5) | copy-start | bytes 49156
  4.7 28.1 %all-to-all-start = ((bf16[64,2,240]{2,1,0:T(2,128)(2,1)}), bf16[64,2,240]{2,1,0:T(2,128)(2,1)S(1)}, u32[]{:S(2)}, u32[]{:S(2)}) async-start(bf16[64,2,240]{2,1,0:T(2,128)(2,1)} %reshape.735), calls=%async_computation | async-start | bytes 131072 | tf_op jit(solution)/shard_map/all_to_all | solution.py:75
  33.8 1.7 %copy-start.1 = (bf16[16,2048]{1,0:T(8,128)(2,1)S(1)}, bf16[16,2048]{1,0:T(8,128)(2,1)}, u32[]{:S(2)}) copy-start(bf16[16,2048]{1,0:T(8,128)(2,1)} %param.9) | copy-start | bytes 196612
  71.1 23.5 %all-to-all-start.1 = ((f32[64,8,108]{2,1,0:T(8,128)}), f32[64,8,108]{2,1,0:T(8,128)S(1)}, u32[]{:S(2)}, u32[]{:S(2)}) async-start(f32[64,8,108]{2,1,0:T(8,128)} %reshape.717), calls=%async_computation.1 | async-start | bytes 524288 | tf_op jit(solution)/shard_map/all_to_all | solution.py:110
